TPU v7x, 256 devices: a whole 4x4x8 slice. The times are simulated.
256 devices in a mesh: dp: 8 (over x, core), expert: 32 (over y, z).
Axes of the slice: x: 4, y: 4, z: 8, core: 2. Of those that a mesh axis runs over, the one named last changes fastest.
Arguments:
- tokens: bfloat16 [4096, 3584], P('expert'), may hold values from -6 to 6
- cotangent: bfloat16 [4096, 3584], P('expert'), may hold values from -0.59765625 to 0.59765625
- route_ids: int32 [4096, 8], P('expert'), may hold values from 0 to 31, all different within a row; in each aligned block of 128 rows (0 to 127, 128 to 255, ...) at most 40 rows name the same one
- route_gates: float32 [4096, 8], P('expert'), may hold values from 0.02 to 0.5
- w_gate: bfloat16 [32, 1792, 3584], P('expert', 'dp'), may hold values from -0.09375 to 0.09375
- w_up: bfloat16 [32, 1792, 3584], P('expert', 'dp'), may hold values from -0.09375 to 0.09375
- w_down: bfloat16 [32, 1792, 3584], P('expert', 'dp'), may hold values from -0.125 to 0.125
Outputs:
- layer_out: bfloat16 [4096, 3584], P(('expert', 'dp'))
- gate_grad: float32 [4096, 8], P(('expert', 'dp'))
- grad_w_gate: bfloat16 [32, 1792, 3584], P('expert', 'dp')
- grad_w_up: bfloat16 [32, 1792, 3584], P('expert', 'dp')
- grad_w_down: bfloat16 [32, 1792, 3584], P('expert', 'dp')
Inputs may be any that keep to these rules, and one draw needn't show every extreme that they name: `route_ids`: each row names 8 different experts. Within each aligned block of 128 rows (the tokens of one index of expert) no expert is named more than 40 times, a bound that some block reaches.
All inputs are finite; a program needn't handle non-finite values.
Results may differ from a plain program's by a relative error of at most 0.02.
Values may be sent and summed in bfloat16 or wider, within the bound.
No kernel may reach another device: no remote copies, remote signals or barrier semaphores. Data moves between devices by JAX's collectives and lax.ppermute only.
A program may use at most 128 MiB of HBM per device.

v0:
```python
import jax
import jax.numpy as jnp
from jax import lax
from jax.sharding import PartitionSpec as P


def body(tokens, cotangent, route_ids, route_gates, w_gate, w_up, w_down):
    groups = lax.axis_size("expert")
    dp_count = lax.axis_size("dp")
    tok_rows, width = tokens.shape
    top_slots = route_ids.shape[1]
    cap_rows = min(tok_rows, dp_count * max(1, tok_rows * top_slots * 5 // (4 * groups * dp_count)))
    flat_ids = route_ids.reshape(-1)
    onehot = (flat_ids[:, None] == jnp.arange(groups, dtype=jnp.int32)[None, :]).astype(jnp.int32)
    slot_rank = jnp.sum(jnp.cumsum(onehot, axis=0) * onehot, axis=1) - 1
    rows_x = jnp.repeat(tokens, top_slots, axis=0)
    scaled = (route_gates[:, :, None] * cotangent[:, None, :].astype(jnp.float32)).astype(
        jnp.bfloat16
    )
    scaled = scaled.reshape(tok_rows * top_slots, width)
    send_x = jnp.zeros((groups, cap_rows, width), jnp.bfloat16).at[flat_ids, slot_rank].set(rows_x)
    send_dy = jnp.zeros((groups, cap_rows, width), jnp.bfloat16).at[flat_ids, slot_rank].set(scaled)
    recv_x, recv_dy = (
        lax.all_to_all(send_x, "expert", split_axis=0, concat_axis=0, tiled=True),
        lax.all_to_all(send_dy, "expert", split_axis=0, concat_axis=0, tiled=True),
    )
    rows_all = groups * cap_rows
    flat_x = recv_x.reshape(rows_all, width)
    flat_dy = recv_dy.reshape(rows_all, width)
    gate_local = w_gate[0]
    up_local = w_up[0]
    down_local = w_down[0]
    by_feature = (((1,), (1,)), ((), ()))
    by_row = (((0,), (0,)), ((), ()))
    gate_pre = lax.dot_general(flat_x, gate_local, by_feature, preferred_element_type=jnp.float32)
    up_pre = lax.dot_general(flat_x, up_local, by_feature, preferred_element_type=jnp.float32)
    sigma_gate = jax.nn.sigmoid(gate_pre)
    hidden = (gate_pre * sigma_gate * up_pre).astype(jnp.bfloat16)
    y_part = jnp.dot(hidden, down_local, preferred_element_type=jnp.float32).astype(jnp.bfloat16)
    hidden_grad = lax.dot_general(
        flat_dy, down_local, by_feature, preferred_element_type=jnp.float32
    )
    grad_gate_pre = (
        hidden_grad * up_pre * sigma_gate * (1.0 + gate_pre * (1.0 - sigma_gate))
    ).astype(jnp.bfloat16)
    grad_up_pre = (hidden_grad * gate_pre * sigma_gate).astype(jnp.bfloat16)
    grad_down = lax.dot_general(hidden, flat_dy, by_row, preferred_element_type=jnp.float32)
    grad_gate = lax.dot_general(grad_gate_pre, flat_x, by_row, preferred_element_type=jnp.float32)
    grad_up = lax.dot_general(grad_up_pre, flat_x, by_row, preferred_element_type=jnp.float32)
    y_flat, grad_gate, grad_up, grad_down = (y_part, grad_gate, grad_up, grad_down)
    y_home = lax.all_to_all(
        y_flat.reshape(groups, cap_rows, width), "expert", split_axis=0, concat_axis=0, tiled=True
    )
    y_slots = y_home[flat_ids, slot_rank].reshape(tok_rows, top_slots, width)
    out_part = jnp.einsum("tk,tkd->td", route_gates, y_slots, preferred_element_type=jnp.float32)
    grad_part = jnp.einsum("td,tkd->tk", cotangent, y_slots, preferred_element_type=jnp.float32)
    layer_sum, gate_sum = (
        lax.psum_scatter(
            out_part.astype(jnp.bfloat16), "dp", scatter_dimension=0, tiled=True
        ).astype(jnp.float32),
        lax.psum_scatter(
            grad_part.astype(jnp.bfloat16), "dp", scatter_dimension=0, tiled=True
        ).astype(jnp.float32),
    )
    return (
        layer_sum.astype(jnp.bfloat16),
        gate_sum,
        grad_gate.astype(jnp.bfloat16)[None],
        grad_up.astype(jnp.bfloat16)[None],
        grad_down.astype(jnp.bfloat16)[None],
    )


def solution(mesh):
    return jax.shard_map(
        body,
        mesh=mesh,
        in_specs=(
            P("expert", None),
            P("expert", None),
            P("expert", None),
            P("expert", None),
            P("expert", "dp", None),
            P("expert", "dp", None),
            P("expert", "dp", None),
        ),
        out_specs=(
            P(("expert", "dp"), None),
            P(("expert", "dp"), None),
            P("expert", "dp", None),
            P("expert", "dp", None),
            P("expert", "dp", None),
        ),
        check_vma=False,
    )
```

profile of v0, /device:TPU:8, one launch (start us, length us, event | category | flops | bytes accessed | tf_op | source)
XLA Modules:
  0.0 822.7 jit_solution(7863905984933608506)
XLA Ops:
  7.2 0.0 copy-start
  7.2 0.0 copy-start.2
  7.2 0.9 copy.18
  8.1 0.1 eq.29
  8.2 0.1 eq.25
  8.3 0.1 reshape.100
  8.4 9.0 %reduce-window.6 = s32[32,8,128]{2,1,0:T(8,128)S(1)} reduce-window(s32[32,8,128]{2,1,0:T(8,128)S(1)} %fusion.29, s32[]{:T(128)} %constant.7.clone.1), window={size=1x1x128 pad=0_0x0_0x127_0}, to_apply=%region_0.0 | reduce-window | flops 4161536 | bytes 262148 | tf_op jit(solution)/shard_map/reduce-window
  17.4 0.1 slice.10
  17.5 0.1 copy.21
  17.7 0.1 copy.22
  17.8 0.1 broadcast_add_fusion
  18.0 0.8 and_reduce_fusion
  18.7 0.7 multiply_reduce_fusion
  19.5 0.0 copy-done.2
  19.5 15.2 %scatter_custom_fusion = bf16[1280,3584]{1,0:T(8,128)(2,1)} fusion(s32[1024]{0:T(1024)S(1)} %broadcast_select_fusion, bf16[]{:T(256)} %constant.6.clone.1, bf16[128,3584]{1,0:T(8,128)(2,1)S(1)} %copy-done.2), kind=kCustom, calls=%fused_computation.11 | custom fusion | bytes 10092546
  34.7 0.0 copy-start.4
  34.7 12.5 %all-to-all-start = ((bf16[32,40,3584]{2,1,0:T(8,128)(2,1)}), bf16[32,40,3584]{2,1,0:T(8,128)(2,1)}, u32[]{:S(2)}, u32[]{:S(2)}) async-start(bf16[32,40,3584]{2,1,0:T(8,128)(2,1)} %bitcast.77), calls=%async_computation | async-start | bytes 18350080 | tf_op jit(solution)/shard_map/all_to_all | solution.py:24
  47.3 0.0 copy-done.4
  47.3 0.1 copy.23
  47.4 0.1 mul.48
  47.5 1.4 convert_element_type.51
  48.8 15.7 %scatter_custom_fusion.1 = bf16[1280,3584]{1,0:T(8,128)(2,1)} fusion(s32[1024]{0:T(1024)S(1)} %broadcast_select_fusion, f32[128,3584]{1,0:T(8,128)S(1)} %convert_element_type.51, f32[1024]{0:T(1024)S(1)} %mul.48, bf16[]{:T(256)} %constant.6.clone.1), kind=kCustom, calls=%fused_computation.6 | custom fusion | flops 7340032 | bytes 11014146
  64.5 187.5 %all-to-all-done = bf16[32,40,3584]{2,1,0:T(8,128)(2,1)} async-done(((bf16[32,40,3584]{2,1,0:T(8,128)(2,1)}), bf16[32,40,3584]{2,1,0:T(8,128)(2,1)}, u32[]{:S(2)}, u32[]{:S(2)}) %all-to-all-start) | async-done | bytes 9175072 | tf_op jit(solution)/shard_map/all_to_all | solution.py:24
  252.0 0.0 copy-start.5
  252.0 19.5 %all-to-all-start.2 = ((bf16[32,40,3584]{2,1,0:T(8,128)(2,1)}), bf16[32,40,3584]{2,1,0:T(8,128)(2,1)}, u32[]{:S(2)}, u32[]{:S(2)}) async-start(bf16[32,40,3584]{2,1,0:T(8,128)(2,1)} %bitcast.76), calls=%async_computation.3 | async-start | bytes 18350080 | tf_op jit(solution)/shard_map/all_to_all | solution.py:25
  271.6 0.0 copy-done.5
  271.6 0.0 copy-start.6
  271.6 6.6 fusion.23
  278.1 0.0 copy-done.6
  278.2 0.0 copy-start.7
  278.2 7.9 multiply_convert_fusion.2
  286.1 0.0 copy-done.7
  286.1 0.0 copy-done
  286.1 6.1 convolution_convert_fusion
  292.2 179.7 %all-to-all-done.2 = bf16[32,40,3584]{2,1,0:T(8,128)(2,1)} async-done(((bf16[32,40,3584]{2,1,0:T(8,128)(2,1)}), bf16[32,40,3584]{2,1,0:T(8,128)(2,1)}, u32[]{:S(2)}, u32[]{:S(2)}) %all-to-all-start.2) | async-done | bytes 9175072 | tf_op jit(solution)/shard_map/all_to_all | solution.py:25
  471.9 22.6 %all-to-all-start.1 = ((bf16[32,40,3584]{2,1,0:T(8,128)(2,1)}), bf16[32,40,3584]{2,1,0:T(8,128)(2,1)}, u32[]{:S(2)}, u32[]{:S(2)}) async-start(bf16[32,40,3584]{2,1,0:T(8,128)(2,1)} %bitcast.75), calls=%async_computation.1 | async-start | bytes 18350080 | tf_op jit(solution)/shard_map/all_to_all | solution.py:51
  494.5 0.0 reduce-scatter.7.cloned.1.call-start
  494.5 0.1 copy.24
  494.7 6.4 fusion.18
  501.1 192.4 %all-to-all-done.1 = bf16[32,40,3584]{2,1,0:T(8,128)(2,1)} async-done(((bf16[32,40,3584]{2,1,0:T(8,128)(2,1)}), bf16[32,40,3584]{2,1,0:T(8,128)(2,1)}, u32[]{:S(2)}, u32[]{:S(2)}) %all-to-all-start.1) | async-done | bytes 9175072 | tf_op jit(solution)/shard_map/all_to_all | solution.py:51
  693.5 0.0 copy-start.3
  693.5 32.1 %gather_fusion = bf16[1024,3584]{1,0:T(8,128)(2,1)} fusion(bf16[32,40,3584]{2,1,0:T(8,128)(2,1)} %all-to-all-done.1, s32[1024]{0:T(1024)S(1)} %bitcast.74), kind=kCustom, calls=%fused_computation | custom fusion | bytes 14688256 | tf_op jit(solution)/shard_map/gather | solution.py:54
  725.6 0.0 copy-done.3
  725.6 7.2 fusion.3
  732.8 0.1 copy.27
  732.9 0.7 copy.28
  733.7 0.0 reduce-scatter.7.cloned.1.call-update
  733.7 0.3 reduce-scatter.5.cloned.1.call-start
  733.9 5.1 fusion.5
  739.1 1.1 copy.35
  740.1 0.0 reduce-scatter.5.cloned.1.call-update
  740.1 0.0 copy-start.8
  740.2 7.1 fusion.13
  747.3 0.0 copy-done.8
  747.3 0.0 copy-start.9
  747.3 7.2 fusion.12
  754.5 0.0 copy-done.9
  754.5 0.0 copy-start.1
  754.5 7.5 fusion.11
  762.0 17.3 %reduce-scatter.7.cloned.1.call-done = bf16[16,8]{1,0:T(8,128)(2,1)} async-done(((bf16[128,8]{1,0:T(8,128)(2,1)}), bf16[16,8]{1,0:T(8,128)(2,1)}) %reduce-scatter.7.cloned.1.call-update) | async-done | bytes 272
  779.3 0.7 copy.29
  780.0 0.6 convert_element_type.50
  780.6 35.0 %reduce-scatter.5.cloned.1.call-done = bf16[16,3584]{1,0:T(8,128)(2,1)} async-done(((bf16[128,3584]{1,0:T(8,128)(2,1)}), bf16[16,3584]{1,0:T(8,128)(2,1)}) %reduce-scatter.5.cloned.1.call-update) | async-done | bytes 114704 | tf_op jit(solution)/shard_map/reduce_scatter | solution.py:58
  815.6 0.0 copy-done.1
  (7 shorter events, 0.1 us)
Async XLA Ops:
  7.2 278.9 %copy-start = (bf16[1,224,3584]{2,1,0:T(8,128)(2,1)S(1)}, bf16[1,224,3584]{2,1,0:T(8,128)(2,1)}, u32[]{:S(2)}) copy-start(bf16[1,224,3584]{2,1,0:T(8,128)(2,1)} %param.13) | copy-start | bytes 4816900
  7.2 12.3 %copy-start.2 = (bf16[128,3584]{1,0:T(8,128)(2,1)S(1)}, bf16[128,3584]{1,0:T(8,128)(2,1)}, u32[]{:S(2)}) copy-start(bf16[128,3584]{1,0:T(8,128)(2,1)} %param.7) | copy-start | bytes 2752516
  34.7 12.5 %copy-start.4 = (f32[128,8]{0,1:T(8,128)S(1)}, f32[128,8]{0,1:T(8,128)}, u32[]{:S(2)}) copy-start(f32[128,8]{0,1:T(8,128)} %param.10) | copy-start | bytes 12292
  34.7 217.3 %all-to-all-start = ((bf16[32,40,3584]{2,1,0:T(8,128)(2,1)}), bf16[32,40,3584]{2,1,0:T(8,128)(2,1)}, u32[]{:S(2)}, u32[]{:S(2)}) async-start(bf16[32,40,3584]{2,1,0:T(8,128)(2,1)} %bitcast.77), calls=%async_computation | async-start | bytes 18350080 | tf_op jit(solution)/shard_map/all_to_all | solution.py:24
  252.0 19.6 %copy-start.5 = (bf16[1,224,3584]{2,1,0:T(8,128)(2,1)S(1)}, bf16[1,224,3584]{2,1,0:T(8,128)(2,1)}, u32[]{:S(2)}) copy-start(bf16[1,224,3584]{2,1,0:T(8,128)(2,1)} %param.11) | copy-start | bytes 4816900
  252.0 219.9 %all-to-all-start.2 = ((bf16[32,40,3584]{2,1,0:T(8,128)(2,1)}), bf16[32,40,3584]{2,1,0:T(8,128)(2,1)}, u32[]{:S(2)}, u32[]{:S(2)}) async-start(bf16[32,40,3584]{2,1,0:T(8,128)(2,1)} %bitcast.76), calls=%async_computation.3 | async-start | bytes 18350080 | tf_op jit(solution)/shard_map/all_to_all | solution.py:25
  271.6 6.6 copy-start.6
  278.2 7.9 copy-start.7
  471.9 221.7 %all-to-all-start.1 = ((bf16[32,40,3584]{2,1,0:T(8,128)(2,1)}), bf16[32,40,3584]{2,1,0:T(8,128)(2,1)}, u32[]{:S(2)}, u32[]{:S(2)}) async-start(bf16[32,40,3584]{2,1,0:T(8,128)(2,1)} %bitcast.75), calls=%async_computation.1 | async-start | bytes 18350080 | tf_op jit(solution)/shard_map/all_to_all | solution.py:51
  494.5 284.8 %reduce-scatter.7.cloned.1.call-start = ((), (), s32[]{:S(2)}) async-start(), calls=%async_computation.6 | async-start | bytes 36864
  693.5 32.1 %copy-start.3 = (bf16[128,3584]{1,0:T(8,128)(2,1)S(1)}, bf16[128,3584]{1,0:T(8,128)(2,1)}, u32[]{:S(2)}) copy-start(bf16[128,3584]{1,0:T(8,128)(2,1)} %param.8) | copy-start | bytes 2752516
  733.7 82.0 %reduce-scatter.5.cloned.1.call-start = ((), (), s32[]{:S(2)}) async-start(), calls=%async_computation.5 | async-start | bytes 1032192 | tf_op jit(solution)/shard_map/reduce_scatter | solution.py:58
  740.1 7.1 copy-start.8
  747.3 7.2 copy-start.9
  754.5 61.2 %copy-start.1 = (bf16[1,224,3584]{2,1,0:T(8,128)(2,1)S(1)}, bf16[1,224,3584]{2,1,0:T(8,128)(2,1)}, u32[]{:S(2)}) copy-start(bf16[1,224,3584]{2,1,0:T(8,128)(2,1)} %param.13) | copy-start | bytes 4816900
Sparse Core Ops, SparseCore 0:
  733.8 45.4 reduce-scatter.6
  782.4 33.1 reduce-scatter.4
where the time goes:
time: 831 us; the launch traced here: 823 us
  waiting for transfers between devices  612 us (74%)
  matrix products  61.2 us (7%)
  starting transfers between devices  55 us (7%)
  local copies, waits for them, and re-layouts  51.8 us (6%)
  other arithmetic  28.4 us (3%)
  between operations  14.5 us (2%)
    all_to_all x1, waiting for transfers between devices, body(): lax.all_to_all(y_flat.reshape(groups, cap_rows, width), 'expert', split_a...  192 us
    all_to_all x1, waiting for transfers between devices, body(): lax.all_to_all(send_x, 'expert', split_axis=0, concat_axis=0, tiled=True)  187 us
    all_to_all x1, waiting for transfers between devices, body(): lax.all_to_all(send_dy, 'expert', split_axis=0, concat_axis=0, tiled=True)  180 us
    reduce_scatter x1, waiting for transfers between devices, body(): lax.psum_scatter(out_part.astype(jnp.bfloat16), 'dp', scatter_dimension=0...  35 us
    gather x1, local copies, waits for them, and re-layouts, body(): y_slots = y_home[flat_ids, slot_rank].reshape(tok_rows, top_slots, width)  32.1 us
    all_to_all x1, starting transfers between devices, body(): lax.all_to_all(y_flat.reshape(groups, cap_rows, width), 'expert', split_a...  22.6 us
    all_to_all x1, starting transfers between devices, body(): lax.all_to_all(send_dy, 'expert', split_axis=0, concat_axis=0, tiled=True)  19.5 us
    unnamed x26, local copies, waits for them, and re-layouts  18 us
  transfers between devices with their start and end apart: 5, of which 5 were waited for; matrix products, arithmetic and copies ran while one was open for 9% of the time, Pallas kernels for 0%

commit v1 on v0

v1 whole, which is shorter than its diff:
```python
import jax
import jax.numpy as jnp
from jax import lax
from jax.sharding import PartitionSpec as P


def body(tokens, cotangent, route_ids, route_gates, w_gate, w_up, w_down):
    groups = lax.axis_size("expert")
    dp_count = lax.axis_size("dp")
    dp_idx = lax.axis_index("dp")
    tok_rows, width = tokens.shape
    top_slots = route_ids.shape[1]
    cap_rows = min(tok_rows, dp_count * max(1, tok_rows * top_slots * 5 // (4 * groups * dp_count)))
    share = cap_rows // dp_count
    n_dest = groups * share
    flat_ids = route_ids.reshape(-1)
    onehot = (flat_ids[:, None] == jnp.arange(groups, dtype=jnp.int32)[None, :]).astype(jnp.int32)
    slot_rank = jnp.sum(jnp.cumsum(onehot, axis=0) * onehot, axis=1) - 1
    local_rank = slot_rank - dp_idx * share
    mine = (local_rank >= 0) & (local_rank < share)
    dest = jnp.where(mine, flat_ids * share + local_rank, n_dest)
    dest_hot = (dest[:, None] == jnp.arange(n_dest, dtype=jnp.int32)[None, :]).astype(jnp.float32)
    pick = jnp.sum(dest_hot.reshape(tok_rows, top_slots, n_dest), axis=1).T
    pick_bf = pick.astype(jnp.bfloat16)
    gate_sel = jnp.sum(dest_hot * route_gates.reshape(-1)[:, None], axis=0)
    send_x = jnp.dot(pick_bf, tokens, preferred_element_type=jnp.float32).astype(jnp.bfloat16)
    cot_sel = jnp.dot(pick_bf, cotangent, preferred_element_type=jnp.float32)
    send_dy = (gate_sel[:, None] * cot_sel).astype(jnp.bfloat16)
    recv_x = lax.all_to_all(
        send_x.reshape(groups, share, width), "expert", split_axis=0, concat_axis=0, tiled=True
    )
    recv_dy = lax.all_to_all(
        send_dy.reshape(groups, share, width), "expert", split_axis=0, concat_axis=0, tiled=True
    )
    rows_all = dp_count * groups * share
    flat_x = lax.all_gather(recv_x, "dp", axis=0, tiled=False).reshape(rows_all, width)
    flat_dy = lax.all_gather(recv_dy, "dp", axis=0, tiled=False).reshape(rows_all, width)
    gate_local = w_gate[0]
    up_local = w_up[0]
    down_local = w_down[0]
    by_feature = (((1,), (1,)), ((), ()))
    by_row = (((0,), (0,)), ((), ()))
    gate_pre = lax.dot_general(flat_x, gate_local, by_feature, preferred_element_type=jnp.float32)
    up_pre = lax.dot_general(flat_x, up_local, by_feature, preferred_element_type=jnp.float32)
    sigma_gate = jax.nn.sigmoid(gate_pre)
    hidden = (gate_pre * sigma_gate * up_pre).astype(jnp.bfloat16)
    y_part = jnp.dot(hidden, down_local, preferred_element_type=jnp.float32).astype(jnp.bfloat16)
    hidden_grad = lax.dot_general(
        flat_dy, down_local, by_feature, preferred_element_type=jnp.float32
    )
    grad_gate_pre = (
        hidden_grad * up_pre * sigma_gate * (1.0 + gate_pre * (1.0 - sigma_gate))
    ).astype(jnp.bfloat16)
    grad_up_pre = (hidden_grad * gate_pre * sigma_gate).astype(jnp.bfloat16)
    grad_down = lax.dot_general(hidden, flat_dy, by_row, preferred_element_type=jnp.float32)
    grad_gate = lax.dot_general(grad_gate_pre, flat_x, by_row, preferred_element_type=jnp.float32)
    grad_up = lax.dot_general(grad_up_pre, flat_x, by_row, preferred_element_type=jnp.float32)
    y_sum = lax.psum_scatter(
        y_part.astype(jnp.float32).reshape(dp_count, groups * share, width),
        "dp",
        scatter_dimension=0,
        tiled=False,
    )
    y_home = lax.all_to_all(
        y_sum.reshape(groups, share, width), "expert", split_axis=0, concat_axis=0, tiled=True
    ).reshape(n_dest, width)
    out_part = lax.dot_general(
        pick,
        gate_sel[:, None] * y_home,
        by_row,
        precision=lax.Precision.HIGHEST,
        preferred_element_type=jnp.float32,
    )
    dot_dest = jnp.sum(cot_sel * y_home, axis=1)
    dot_ext = jnp.concatenate([dot_dest, jnp.zeros((1,), jnp.float32)])
    grad_part = dot_ext[dest].reshape(tok_rows, top_slots)
    layer_sum = lax.psum_scatter(out_part, "dp", scatter_dimension=0, tiled=True)
    gate_sum = lax.psum_scatter(grad_part, "dp", scatter_dimension=0, tiled=True)
    return (
        layer_sum.astype(jnp.bfloat16),
        gate_sum,
        grad_gate.astype(jnp.bfloat16)[None],
        grad_up.astype(jnp.bfloat16)[None],
        grad_down.astype(jnp.bfloat16)[None],
    )


def solution(mesh):
    return jax.shard_map(
        body,
        mesh=mesh,
        in_specs=(
            P("expert", None),
            P("expert", None),
            P("expert", None),
            P("expert", None),
            P("expert", "dp", None),
            P("expert", "dp", None),
            P("expert", "dp", None),
        ),
        out_specs=(
            P(("expert", "dp"), None),
            P(("expert", "dp"), None),
            P("expert", "dp", None),
            P("expert", "dp", None),
            P("expert", "dp", None),
        ),
        check_vma=False,
    )
```

time: 831 us -> 585 us (0.70)
  waiting for transfers between devices: 612 us -> 303 us
  blocking collectives: 0 us -> 106 us
  starting transfers between devices: 55 us -> 10.7 us
  local copies, waits for them, and re-layouts: 51.8 us -> 80.9 us
  matrix products: 61.2 us -> 43.1 us
    all_to_all x3 -> x1, waiting for transfers between devices: 560 us -> 81.6 us  [body(): lax.all_to_all(y_sum.reshape(groups, share, width), 'expert', split_axis=...]
    all_gather x0 -> x2, waiting for transfers between devices: none -> 109 us  [the longest x1 55.1 us: body(): lax.all_gather(recv_dy, 'dp', axis=0, tiled=False).reshape(rows_all, width)]
    all_to_all x0 -> x2, blocking collectives: none -> 106 us  [the longest x1 54.8 us: body(): lax.all_to_all(send_x.reshape(groups, share, width), 'expert', split_axis...]
    reduce_scatter x1 -> x3, waiting for transfers between devices: 35 us -> 112 us  [the longest x1 102 us: body(): lax.psum_scatter(y_part.astype(jnp.float32).reshape(dp_count, groups * sh...]
    all_to_all x3 -> x1, starting transfers between devices: 54.7 us -> 10.3 us  [body(): lax.all_to_all(y_sum.reshape(groups, share, width), 'expert', split_axis=...]
    reshape x1 -> x6, local copies, waits for them, and re-layouts: 0.1 us -> 37.1 us  [the longest x1 15.1 us: body(): lax.all_gather(recv_x, 'dp', axis=0, tiled=False).reshape(rows_all, width)]
    all_gather x0 -> x2, local copies, waits for them, and re-layouts: none -> 27.5 us  [the longest x1 13.8 us: body(): lax.all_gather(recv_dy, 'dp', axis=0, tiled=False).reshape(rows_all, width)]
    gather x1, local copies, waits for them, and re-layouts: 32.1 us -> 6.82 us  [body(): grad_part = dot_ext[dest].reshape(tok_rows, top_slots)]
  transfers between devices with their start and end apart: 5 -> 6, of which waited for: 5 -> 5; matrix products, arithmetic and copies ran while one was open for 9% -> 2% of each run, Pallas kernels for 0% -> 0%
where the time goes in v1:
time: 585 us; the launch traced here: 582 us
  waiting for transfers between devices  303 us (52%)
  blocking collectives  106 us (18%)
  local copies, waits for them, and re-layouts  80.9 us (14%)
  matrix products  43.1 us (7%)
  other arithmetic  24.3 us (4%)
  between operations  14.1 us (2%)
  starting transfers between devices  10.7 us (2%)
    reduce_scatter x1, waiting for transfers between devices, body(): lax.psum_scatter(y_part.astype(jnp.float32).reshape(dp_count, groups * sh...  102 us
    all_to_all x1, waiting for transfers between devices, body(): lax.all_to_all(y_sum.reshape(groups, share, width), 'expert', split_axis=...  81.6 us
    all_gather x1, waiting for transfers between devices, body(): lax.all_gather(recv_dy, 'dp', axis=0, tiled=False).reshape(rows_all, width)  55.1 us
    all_to_all x1, blocking collectives, body(): lax.all_to_all(send_x.reshape(groups, share, width), 'expert', split_axis...  54.8 us
    all_gather x1, waiting for transfers between devices, body(): lax.all_gather(recv_x, 'dp', axis=0, tiled=False).reshape(rows_all, width)  54.1 us
    all_to_all x1, blocking collectives, body(): lax.all_to_all(send_dy.reshape(groups, share, width), 'expert', split_axi...  50.8 us
    reshape x1, local copies, waits for them, and re-layouts, body(): lax.all_gather(recv_x, 'dp', axis=0, tiled=False).reshape(rows_all, width)  15.1 us
    reshape x1, local copies, waits for them, and re-layouts, body(): lax.all_gather(recv_dy, 'dp', axis=0, tiled=False).reshape(rows_all, width)  15 us
  transfers between devices with their start and end apart: 6, of which 5 were waited for; matrix products, arithmetic and copies ran while one was open for 2% of the time, Pallas kernels for 0%

profile of v1, /device:TPU:8, one launch (start us, length us, event | category | flops | bytes accessed | tf_op | source)
XLA Modules:
  0.0 581.8 jit_solution(15260357586573973833)
XLA Ops:
  7.2 0.0 copy-start
  7.2 0.0 all-gather.5.cloned.1.call-start
  7.2 0.9 copy.31
  8.2 0.1 eq.45
  8.3 0.1 eq.49
  8.4 9.0 %reduce-window.6 = s32[32,8,128]{2,1,0:T(8,128)S(1)} reduce-window(s32[32,8,128]{2,1,0:T(8,128)S(1)} %fusion.17, s32[]{:T(128)} %constant.10.clone.1), window={size=1x1x128 pad=0_0x0_0x127_0}, to_apply=%region_0.0 | reduce-window | flops 4161536 | bytes 262148 | tf_op jit(solution)/shard_map/reduce-window
  17.4 0.1 slice.10
  17.5 0.1 copy.33
  17.7 0.1 copy.34
  17.7 0.1 broadcast_add_fusion
  17.9 0.1 sub.33
  18.0 0.6 broadcast_multiply_fusion
  18.7 0.1 convert_reduce_fusion
  18.8 1.4 convolution_convert_fusion.4
  20.3 1.5 reshape.124
  21.8 54.8 %all_to_all.15 = bf16[32,5,3584]{2,1,0:T(8,128)(2,1)S(1)} all-to-all(bf16[32,5,3584]{2,1,0:T(8,128)(2,1)S(1)} %reshape.124), channel_id=1, replica_groups=mesh['dp'=8,'expert'=32] {'expert'}, dimensions={0} | all-to-all | bytes 2293760 | tf_op jit(solution)/shard_map/all_to_all | solution.py:29
  76.6 1.4 copy.38
  78.0 0.0 all-gather.5.cloned.1.call-update
  78.0 0.0 reduce-scatter.4.cloned.1.call-start
  78.0 54.1 %all-gather.5.cloned.1.call-done = bf16[256,5,3584]{2,0,1:T(8,128)(2,1)} async-done(((bf16[32,5,3584]{2,0,1:T(8,128)(2,1)}), bf16[256,5,3584]{2,0,1:T(8,128)(2,1)}) %all-gather.5.cloned.1.call-update) | async-done | bytes 9175056 | tf_op jit(solution)/shard_map/all_gather | solution.py:36
  132.1 13.8 %copy.39 = bf16[256,5,3584]{2,1,0:T(8,128)(2,1)} copy(bf16[256,5,3584]{2,0,1:T(8,128)(2,1)} %all-gather.5.cloned.1.call-done) | data formatting | bytes 18350080 | tf_op jit(solution)/shard_map/all_gather | solution.py:36
  145.9 15.1 %reshape.125 = bf16[1280,3584]{1,0:T(8,128)(2,1)} reshape(bf16[256,5,3584]{2,1,0:T(8,128)(2,1)} %copy.39) | data formatting | bytes 18350080 | tf_op jit(solution)/shard_map/reshape | solution.py:36
  161.0 6.6 %fusion.10 = f32[1280,224]{0,1:T(8,128)S(1)} fusion(bf16[1280,3584]{1,0:T(8,128)(2,1)} %reshape.125, bf16[1,224,3584]{2,1,0:T(8,128)(2,1)S(1)} %copy-done.9), kind=kOutput, calls=%fused_computation.18 | convolution fusion | flops 2055208960 | bytes 11927552 | tf_op jit(solution)/shard_map/dot_general | solution.py:43
  167.6 0.0 copy-done.10
  167.6 3.9 multiply_convert_fusion.3
  171.5 6.1 %convolution_convert_fusion = bf16[1280,3584]{1,0:T(8,128)(2,1)} fusion(bf16[1280,224]{0,1:T(8,128)(2,1)S(1)} %get-tuple-element.26, bf16[1,224,3584]{2,1,0:T(8,128)(2,1)S(1)} %copy-done), kind=kOutput, calls=%fused_computation.1 | convolution fusion | flops 2059796480 | bytes 11354112 | tf_op jit(solution)/shard_map/dot_general | solution.py:47
  177.6 12.5 %convert.1 = f32[8,160,3584]{2,1,0:T(8,128)} convert(bf16[8,160,3584]{2,1,0:T(8,128)(2,1)} %bitcast.48) | non-fusion elementwise | flops 4587520 | bytes 27525120 | tf_op jit(solution)/shard_map/reshape | solution.py:59
  190.0 0.0 reduce-scatter.4.cloned.1.call-update
  190.1 102.1 %reduce-scatter.4.cloned.1.call-done = f32[1,160,3584]{2,1,0:T(8,128)} async-done(((f32[8,160,3584]{2,1,0:T(8,128)}), f32[1,160,3584]{2,1,0:T(8,128)}) %reduce-scatter.4.cloned.1.call-update) | async-done | bytes 2293776 | tf_op jit(solution)/shard_map/reduce_scatter | solution.py:58
  292.2 3.3 reshape_reduce_scatter.3
  295.5 10.3 %all-to-all-start.1 = ((f32[32,5,3584]{2,1,0:T(8,128)}), f32[32,5,3584]{2,1,0:T(8,128)}, u32[]{:S(2)}, u32[]{:S(2)}) async-start(f32[32,5,3584]{2,1,0:T(8,128)} %reshape_reduce_scatter.3), calls=%async_computation.2 | async-start | bytes 7340032 | tf_op jit(solution)/shard_map/all_to_all | solution.py:64
  305.8 0.2 reduce-scatter.8.cloned.1.call-start
  306.1 0.1 copy.37
  306.2 0.1 mul.80
  306.3 0.1 mul.88
  306.4 0.1 select_reduce_fusion
  306.6 0.0 copy-start.4
  306.6 81.6 %all-to-all-done.1 = f32[32,5,3584]{2,1,0:T(8,128)} async-done(((f32[32,5,3584]{2,1,0:T(8,128)}), f32[32,5,3584]{2,1,0:T(8,128)}, u32[]{:S(2)}, u32[]{:S(2)}) %all-to-all-start.1) | async-done | bytes 2293792 | tf_op jit(solution)/shard_map/all_to_all | solution.py:64
  388.2 3.3 reshape.128
  391.5 3.2 multiply_convert_fusion
  394.7 0.1 pad_maximum_fusion
  394.8 6.8 %gather_fusion = f32[1024]{0:T(1024)S(1)} fusion(f32[161]{0:T(256)S(1)} %pad_maximum_fusion, s32[1024]{0:T(1024)S(1)} %broadcast_clamp_fusion), kind=kCustom, calls=%fused_computation | custom fusion | bytes 12288 | tf_op jit(solution)/shard_map/gather | solution.py:76
  401.6 0.7 reshape.129
  402.4 0.0 reduce-scatter.8.cloned.1.call-update
  402.4 0.0 reduce-scatter.6.cloned.1.call-start
  402.4 4.7 fusion.3
  407.1 0.0 reduce-scatter.6.cloned.1.call-update
  407.2 0.0 all-gather.7.cloned.1.call-start
  407.2 1.5 reshape.130
  408.8 50.8 %all_to_all.16 = bf16[32,5,3584]{2,1,0:T(8,128)(2,1)S(1)} all-to-all(bf16[32,5,3584]{2,1,0:T(8,128)(2,1)S(1)} %reshape.130), channel_id=1, replica_groups=mesh['dp'=8,'expert'=32] {'expert'}, dimensions={0} | all-to-all | bytes 2293760 | tf_op jit(solution)/shard_map/all_to_all | solution.py:32
  459.6 1.4 copy.40
  461.0 0.0 all-gather.7.cloned.1.call-update
  461.0 0.0 reduce-scatter.8.cloned.1.call-done
  461.1 1.4 copy.42
  462.4 10.1 %reduce-scatter.6.cloned.1.call-done = f32[16,3584]{1,0:T(8,128)} async-done(((f32[128,3584]{1,0:T(8,128)}), f32[16,3584]{1,0:T(8,128)}) %reduce-scatter.6.cloned.1.call-update) | async-done | bytes 229392 | tf_op jit(solution)/shard_map/reduce_scatter | solution.py:77
  472.5 1.6 convert_element_type.50
  474.1 55.1 %all-gather.7.cloned.1.call-done = bf16[256,5,3584]{2,0,1:T(8,128)(2,1)} async-done(((bf16[32,5,3584]{2,0,1:T(8,128)(2,1)}), bf16[256,5,3584]{2,0,1:T(8,128)(2,1)}) %all-gather.7.cloned.1.call-update) | async-done | bytes 9175056 | tf_op jit(solution)/shard_map/all_gather | solution.py:37
  529.2 13.8 %copy.41 = bf16[256,5,3584]{2,1,0:T(8,128)(2,1)} copy(bf16[256,5,3584]{2,0,1:T(8,128)(2,1)} %all-gather.7.cloned.1.call-done) | data formatting | bytes 18350080 | tf_op jit(solution)/shard_map/all_gather | solution.py:37
  543.0 15.0 %reshape.131 = bf16[1280,3584]{1,0:T(8,128)(2,1)} reshape(bf16[256,5,3584]{2,1,0:T(8,128)(2,1)} %copy.41) | data formatting | bytes 18350080 | tf_op jit(solution)/shard_map/reshape | solution.py:37
  558.0 7.2 %fusion.2 = bf16[1,224,3584]{2,1,0:T(8,128)(2,1)} fusion(bf16[1280,224]{0,1:T(8,128)(2,1)S(1)} %copy-done.6, bf16[1280,3584]{1,0:T(8,128)(2,1)} %reshape.131), kind=kOutput, calls=%fused_computation.8 | convolution fusion | flops 2056011776 | bytes 11354112 | tf_op jit(solution)/shard_map/dot_general | solution.py:55
  565.1 2.8 fusion.5
  568.0 0.0 copy-start.13
  568.0 3.5 fusion.1
  571.5 3.7 fusion
  (39 shorter events, 0.2 us)
Async XLA Ops:
  7.2 164.3 %copy-start = (bf16[1,224,3584]{2,1,0:T(8,128)(2,1)S(1)}, bf16[1,224,3584]{2,1,0:T(8,128)(2,1)}, u32[]{:S(2)}) copy-start(bf16[1,224,3584]{2,1,0:T(8,128)(2,1)} %param.13) | copy-start | bytes 4816900
  7.2 11.6 %copy-start.3 = (bf16[128,3584]{1,0:T(8,128)(2,1)S(1)}, bf16[128,3584]{1,0:T(8,128)(2,1)}, u32[]{:S(2)}) copy-start(bf16[128,3584]{1,0:T(8,128)(2,1)} %param.7) | copy-start | bytes 2752516
  7.2 124.9 %all-gather.5.cloned.1.call-start = ((), (), s32[]{:S(2)}) async-start(), calls=%async_computation.9 | async-start | bytes 10321920 | tf_op jit(solution)/shard_map/all_gather | solution.py:36
  78.0 214.2 %reduce-scatter.4.cloned.1.call-start = ((), (), s32[]{:S(2)}) async-start(), calls=%async_computation.6 | async-start | bytes 20643840 | tf_op jit(solution)/shard_map/reduce_scatter | solution.py:58
  145.9 15.1 %copy-start.9 = (bf16[1,224,3584]{2,1,0:T(8,128)(2,1)S(1)}, bf16[1,224,3584]{2,1,0:T(8,128)(2,1)}, u32[]{:S(2)}) copy-start(bf16[1,224,3584]{2,1,0:T(8,128)(2,1)} %param.11) | copy-start | bytes 4816900
  161.0 6.6 %copy-start.1 = (bf16[1280,3584]{1,0:T(8,128)(2,1)S(1)}, bf16[1280,3584]{1,0:T(8,128)(2,1)}, u32[]{:S(2)}) copy-start(bf16[1280,3584]{1,0:T(8,128)(2,1)} %reshape.125) | copy-start | bytes 27525124
  161.0 6.6 %copy-start.10 = (bf16[1,224,3584]{2,1,0:T(8,128)(2,1)S(1)}, bf16[1,224,3584]{2,1,0:T(8,128)(2,1)}, u32[]{:S(2)}) copy-start(bf16[1,224,3584]{2,1,0:T(8,128)(2,1)} %param.12) | copy-start | bytes 4816900
  167.6 3.9 copy-start.11
  171.5 6.1 %copy-start.5 = (bf16[1280,224]{0,1:T(8,128)(2,1)}, bf16[1280,224]{0,1:T(8,128)(2,1)S(1)}, u32[]{:S(2)}) copy-start(bf16[1280,224]{0,1:T(8,128)(2,1)S(1)} %get-tuple-element.26) | copy-start | bytes 1720324
  295.5 10.6 %copy-start.8 = (f32[128,8]{0,1:T(8,128)S(1)}, f32[128,8]{0,1:T(8,128)}, u32[]{:S(2)}) copy-start(f32[128,8]{0,1:T(8,128)} %param.10) | copy-start | bytes 12292
  295.5 10.8 %copy-start.7 = (s32[128,8]{1,0:T(8,128)S(1)}, s32[128,8]{1,0:T(8,128)}, u32[]{:S(2)}) copy-start(s32[128,8]{1,0:T(8,128)} %get-tuple-element.24) | copy-start | bytes 12292
  295.5 92.7 %all-to-all-start.1 = ((f32[32,5,3584]{2,1,0:T(8,128)}), f32[32,5,3584]{2,1,0:T(8,128)}, u32[]{:S(2)}, u32[]{:S(2)}) async-start(f32[32,5,3584]{2,1,0:T(8,128)} %reshape_reduce_scatter.3), calls=%async_computation.2 | async-start | bytes 7340032 | tf_op jit(solution)/shard_map/all_to_all | solution.py:64
  305.8 155.2 %reduce-scatter.8.cloned.1.call-start = ((), (), s32[]{:S(2)}) async-start(), calls=%async_computation.8 | async-start | bytes 73728 | tf_op jit(solution)/shard_map/reduce_scatter | solution.py:78
  306.6 84.9 %copy-start.4 = (bf16[128,3584]{1,0:T(8,128)(2,1)S(1)}, bf16[128,3584]{1,0:T(8,128)(2,1)}, u32[]{:S(2)}) copy-start(bf16[128,3584]{1,0:T(8,128)(2,1)} %param.8) | copy-start | bytes 2752516
  402.4 70.1 %reduce-scatter.6.cloned.1.call-start = ((), (), s32[]{:S(2)}) async-start(), calls=%async_computation.7 | async-start | bytes 2064384 | tf_op jit(solution)/shard_map/reduce_scatter | solution.py:77
  407.2 122.1 %all-gather.7.cloned.1.call-start = ((), (), s32[]{:S(2)}) async-start(), calls=%async_computation.10 | async-start | bytes 10321920 | tf_op jit(solution)/shard_map/all_gather | solution.py:37
  543.0 15.0 %copy-start.6 = (bf16[1280,224]{0,1:T(8,128)(2,1)S(1)}, bf16[1280,224]{0,1:T(8,128)(2,1)}, u32[]{:S(2)}) copy-start(bf16[1280,224]{0,1:T(8,128)(2,1)} %copy-done.5) | copy-start | bytes 1720324
  558.0 7.2 %copy-start.2 = (bf16[1280,3584]{1,0:T(8,128)(2,1)S(1)}, bf16[1280,3584]{1,0:T(8,128)(2,1)}, u32[]{:S(2)}) copy-start(bf16[1280,3584]{1,0:T(8,128)(2,1)} %reshape.131) | copy-start | bytes 27525124
  558.0 10.0 %slice-start = ((s8[9175040]{0:T(1024)(128)(4,1)}), s8[4194304]{0:T(1024)(128)(4,1)S(1)}, s32[]{:S(2)}) async-start(s8[9175040]{0:T(1024)(128)(4,1)} %bitcast.49), calls=%async_computation.11 | async-start | bytes 8388608
  558.0 10.0 %slice-start.1 = ((s8[9175040]{0:T(1024)(128)(4,1)}), s8[4194304]{0:T(1024)(128)(4,1)S(1)}, s32[]{:S(2)}) async-start(s8[9175040]{0:T(1024)(128)(4,1)} %bitcast.49), calls=%async_computation.12 | async-start | bytes 8388608
  565.1 2.9 slice-start.2
  565.1 2.9 copy-start.12
  568.0 3.5 copy-start.13
Sparse Core Ops, SparseCore 0:
  78.1 53.9 all-gather.4
  190.2 101.9 reduce-scatter.3
  402.5 32.3 reduce-scatter.7
  437.3 35.0 reduce-scatter.5
  474.7 54.4 all-gather.6

commit v2 on v1

--- a/solution.py
+++ b/solution.py
@@ -18,7 +18,7 @@
     slot_rank = jnp.sum(jnp.cumsum(onehot, axis=0) * onehot, axis=1) - 1
     local_rank = slot_rank - dp_idx * share
     mine = (local_rank >= 0) & (local_rank < share)
-    dest = jnp.where(mine, flat_ids * share + local_rank, n_dest)
+    dest = jnp.where(mine, local_rank * groups + flat_ids, n_dest)
     dest_hot = (dest[:, None] == jnp.arange(n_dest, dtype=jnp.int32)[None, :]).astype(jnp.float32)
     pick = jnp.sum(dest_hot.reshape(tok_rows, top_slots, n_dest), axis=1).T
     pick_bf = pick.astype(jnp.bfloat16)
@@ -26,15 +26,21 @@
     send_x = jnp.dot(pick_bf, tokens, preferred_element_type=jnp.float32).astype(jnp.bfloat16)
     cot_sel = jnp.dot(pick_bf, cotangent, preferred_element_type=jnp.float32)
     send_dy = (gate_sel[:, None] * cot_sel).astype(jnp.bfloat16)
-    recv_x = lax.all_to_all(
-        send_x.reshape(groups, share, width), "expert", split_axis=0, concat_axis=0, tiled=True
-    )
-    recv_dy = lax.all_to_all(
-        send_dy.reshape(groups, share, width), "expert", split_axis=0, concat_axis=0, tiled=True
-    )
-    rows_all = dp_count * groups * share
-    flat_x = lax.all_gather(recv_x, "dp", axis=0, tiled=False).reshape(rows_all, width)
-    flat_dy = lax.all_gather(recv_dy, "dp", axis=0, tiled=False).reshape(rows_all, width)
+
+    def to_lanes(rows):
+        return jnp.concatenate(
+            [rows[r * groups : (r + 1) * groups] for r in range(share)], axis=1
+        )
+
+    def lanes_to_rows(packed):
+        return jnp.concatenate(
+            [packed[:, r * width : (r + 1) * width] for r in range(share)], axis=0
+        )
+
+    recv_x = lax.all_to_all(to_lanes(send_x), "expert", split_axis=0, concat_axis=0, tiled=True)
+    recv_dy = lax.all_to_all(to_lanes(send_dy), "expert", split_axis=0, concat_axis=0, tiled=True)
+    flat_x = lanes_to_rows(lax.all_gather(recv_x, "dp", axis=0, tiled=True))
+    flat_dy = lanes_to_rows(lax.all_gather(recv_dy, "dp", axis=0, tiled=True))
     gate_local = w_gate[0]
     up_local = w_up[0]
     down_local = w_down[0]
@@ -55,15 +61,13 @@
     grad_down = lax.dot_general(hidden, flat_dy, by_row, preferred_element_type=jnp.float32)
     grad_gate = lax.dot_general(grad_gate_pre, flat_x, by_row, preferred_element_type=jnp.float32)
     grad_up = lax.dot_general(grad_up_pre, flat_x, by_row, preferred_element_type=jnp.float32)
-    y_sum = lax.psum_scatter(
-        y_part.astype(jnp.float32).reshape(dp_count, groups * share, width),
-        "dp",
-        scatter_dimension=0,
-        tiled=False,
+    stack_rows = dp_count * groups
+    y_lanes = jnp.concatenate(
+        [y_part[r * stack_rows : (r + 1) * stack_rows] for r in range(share)], axis=1
     )
-    y_home = lax.all_to_all(
-        y_sum.reshape(groups, share, width), "expert", split_axis=0, concat_axis=0, tiled=True
-    ).reshape(n_dest, width)
+    y_sum = lax.psum_scatter(y_lanes, "dp", scatter_dimension=0, tiled=True)
+    y_back = lax.all_to_all(y_sum, "expert", split_axis=0, concat_axis=0, tiled=True)
+    y_home = lanes_to_rows(y_back).astype(jnp.float32)
     out_part = lax.dot_general(
         pick,
         gate_sel[:, None] * y_home,

time: 585 us -> 424 us (0.72)
  waiting for transfers between devices: 303 us -> 201 us
  blocking collectives: 106 us -> 81 us
  matrix products: 43.1 us -> 27.9 us
  local copies, waits for them, and re-layouts: 80.9 us -> 67.3 us
    all_to_all x1, waiting for transfers between devices: 81.6 us -> 27.1 us  [body(): lax.all_to_all(y_sum, 'expert', split_axis=0, concat_axis=0, tiled=True)]
    unnamed x37 -> x62, local copies, waits for them, and re-layouts: 2.49 us -> 46.3 us
    reduce_scatter x1, waiting for transfers between devices: 102 us -> 59.1 us  [body(): y_sum = lax.psum_scatter(y_lanes, 'dp', scatter_dimension=0, tiled=True)]
    reshape x5 -> x1, local copies, waits for them, and re-layouts: 36.4 us -> 0.1 us  [body(): flat_ids = route_ids.reshape(-1)]
    all_gather x2 -> x0, local copies, waits for them, and re-layouts: 27.5 us -> none  [the longest x1 13.8 us: body(): lax.all_gather(recv_dy, 'dp', axis=0, tiled=False).reshape(rows_all, width)]
    all_to_all x2, blocking collectives: 106 us -> 81 us  [the longest x1 42.8 us: body(): lax.all_to_all(to_lanes(send_x), 'expert', split_axis=0, concat_axis=0, t...]
    reshape x1 -> x0, other arithmetic: 12.5 us -> none  [body(): y_part.astype(jnp.float32).reshape(dp_count, groups * share, width)]
    all_to_all x0 -> x3, other arithmetic: none -> 8.34 us  [the longest x1 2.78 us: body(): lax.all_to_all(to_lanes(send_dy), 'expert', split_axis=0, concat_axis=0,...]
  transfers between devices with their start and end apart: 6 -> 6, of which waited for: 5 -> 5; matrix products, arithmetic and copies ran while one was open for 2% -> 6% of each run, Pallas kernels for 0% -> 0%
where the time goes in v2:
time: 424 us; the launch traced here: 421 us
  waiting for transfers between devices  201 us (47%)
  blocking collectives  81 us (19%)
  local copies, waits for them, and re-layouts  67.3 us (16%)
  matrix products  27.9 us (7%)
  other arithmetic  19.5 us (5%)
  between operations  14.2 us (3%)
  starting transfers between devices  10.7 us (3%)
    reduce_scatter x1, waiting for transfers between devices, body(): y_sum = lax.psum_scatter(y_lanes, 'dp', scatter_dimension=0, tiled=True)  59.1 us
    all_gather x1, waiting for transfers between devices, body(): flat_dy = lanes_to_rows(lax.all_gather(recv_dy, 'dp', axis=0, tiled=True))  55.1 us
    all_gather x1, waiting for transfers between devices, body(): flat_x = lanes_to_rows(lax.all_gather(recv_x, 'dp', axis=0, tiled=True))  51.5 us
    unnamed x62, local copies, waits for them, and re-layouts  46.3 us
    all_to_all x1, blocking collectives, body(): lax.all_to_all(to_lanes(send_x), 'expert', split_axis=0, concat_axis=0, t...  42.8 us
    all_to_all x1, blocking collectives, body(): lax.all_to_all(to_lanes(send_dy), 'expert', split_axis=0, concat_axis=0,...  38.2 us
    all_to_all x1, waiting for transfers between devices, body(): lax.all_to_all(y_sum, 'expert', split_axis=0, concat_axis=0, tiled=True)  27.1 us
    all_to_all x1, starting transfers between devices, body(): lax.all_to_all(y_sum, 'expert', split_axis=0, concat_axis=0, tiled=True)  10.3 us
  transfers between devices with their start and end apart: 6, of which 5 were waited for; matrix products, arithmetic and copies ran while one was open for 6% of the time, Pallas kernels for 0%

profile of v2, /device:TPU:8, one launch (start us, length us, event | category | flops | bytes accessed | tf_op | source)
XLA Modules:
  0.0 421.2 jit_solution(13562572381809185277)
XLA Ops:
  7.2 0.9 copy.45
  8.4 9.0 %reduce-window.6 = s32[32,8,128]{2,1,0:T(8,128)S(1)} reduce-window(s32[32,8,128]{2,1,0:T(8,128)S(1)} %fusion.17, s32[]{:T(128)} %constant.11.clone.1), window={size=1x1x128 pad=0_0x0_0x127_0}, to_apply=%region_0.0 | reduce-window | flops 4161536 | bytes 262148 | tf_op jit(solution)/shard_map/reduce-window
  17.5 0.1 copy.47
  18.3 0.4 convolution_convert_fusion.4
  18.9 1.0 copy-done.1
  19.9 0.5 broadcast.164
  20.4 2.8 reduce
  23.2 1.2 reshape.135
  24.3 42.8 %all_to_all.36 = bf16[32,2,8960]{2,1,0:T(2,128)(2,1)S(1)} all-to-all(bf16[32,2,8960]{2,1,0:T(2,128)(2,1)} %reshape.135), channel_id=1, replica_groups=mesh['dp'=8,'expert'=32] {'expert'}, dimensions={0} | all-to-all | bytes 2293760 | tf_op jit(solution)/shard_map/all_to_all | solution.py:40
  67.1 3.4 reshape.136
  70.5 2.8 copy.53
  73.4 51.5 %all-gather.5.cloned.1.call-done = bf16[256,1,17920]{2,0,1:T(8,128)(2,1)} async-done(((bf16[32,1,17920]{2,0,1:T(8,128)(2,1)}), bf16[256,1,17920]{2,0,1:T(8,128)(2,1)}) %all-gather.5.cloned.1.call-update) | async-done | bytes 9175056 | tf_op jit(solution)/shard_map/all_gather | solution.py:42
  124.9 1.6 slice_dynamic-update-slice_fusion.14
  126.5 1.6 slice_dynamic-update-slice_fusion.13
  128.1 1.6 slice_dynamic-update-slice_fusion.12
  129.7 1.6 slice_dynamic-update-slice_fusion.11
  131.4 1.7 slice_dynamic-update-slice_fusion.10
  133.1 0.2 copy-done.6
  133.3 2.8 fusion.10
  136.2 0.8 copy-done.4
  136.9 3.9 multiply_convert_fusion.3
  140.8 2.6 convolution_convert_fusion
  143.4 1.4 slice_dynamic-update-slice_fusion.9
  144.8 1.4 slice_dynamic-update-slice_fusion.8
  146.2 1.4 slice_dynamic-update-slice_fusion.7
  147.7 1.4 slice_dynamic-update-slice_fusion.6
  149.0 1.4 slice_dynamic-update-slice_fusion.5
  150.5 59.1 %reduce-scatter.4.cloned.1.call-done = bf16[32,17920]{1,0:T(8,128)(2,1)} async-done(((bf16[256,17920]{1,0:T(8,128)(2,1)}), bf16[32,17920]{1,0:T(8,128)(2,1)}) %reduce-scatter.4.cloned.1.call-update) | async-done | bytes 1146896 | tf_op jit(solution)/shard_map/reduce_scatter | solution.py:68
  209.6 2.8 reduce.1
  212.4 1.2 reshape.137
  213.6 10.3 %all-to-all-start.1 = ((bf16[32,2,8960]{2,1,0:T(2,128)(2,1)}), bf16[32,2,8960]{2,1,0:T(2,128)(2,1)S(1)}, u32[]{:S(2)}, u32[]{:S(2)}) async-start(bf16[32,2,8960]{2,1,0:T(2,128)(2,1)} %reshape.137), calls=%async_computation.2 | async-start | bytes 2293760 | tf_op jit(solution)/shard_map/all_to_all | solution.py:69
  223.9 0.2 reduce-scatter.8.cloned.1.call-start
  224.4 0.2 select_reduce_fusion
  224.6 27.1 %all-to-all-done.1 = bf16[32,2,8960]{2,1,0:T(2,128)(2,1)S(1)} async-done(((bf16[32,2,8960]{2,1,0:T(2,128)(2,1)}), bf16[32,2,8960]{2,1,0:T(2,128)(2,1)S(1)}, u32[]{:S(2)}, u32[]{:S(2)}) %all-to-all-start.1) | async-done | bytes 1146912 | tf_op jit(solution)/shard_map/all_to_all | solution.py:69
  251.7 3.4 reshape.138
  255.1 1.8 copy.63
  257.0 1.0 copy-done.3
  258.0 1.6 multiply_convert_fusion
  259.8 6.8 %gather_fusion = f32[1024]{0:T(1024)S(1)} fusion(f32[161]{0:T(256)S(1)} %pad_maximum_fusion, s32[1024]{0:T(1024)S(1)} %broadcast_clamp_fusion), kind=kCustom, calls=%fused_computation | custom fusion | bytes 12288 | tf_op jit(solution)/shard_map/gather | solution.py:80
  266.6 0.7 reshape.124
  267.4 1.7 slice_dynamic-update-slice_fusion.19
  269.0 1.7 slice_dynamic-update-slice_fusion.18
  270.7 1.6 slice_dynamic-update-slice_fusion.17
  272.3 3.1 fusion.3
  275.5 1.6 slice_dynamic-update-slice_fusion.16
  277.1 1.7 slice_dynamic-update-slice_fusion.15
  278.8 2.8 reduce.2
  281.6 1.2 reshape.139
  282.7 38.2 %all_to_all.37 = bf16[32,2,8960]{2,1,0:T(2,128)(2,1)S(1)} all-to-all(bf16[32,2,8960]{2,1,0:T(2,128)(2,1)} %reshape.139), channel_id=1, replica_groups=mesh['dp'=8,'expert'=32] {'expert'}, dimensions={0} | all-to-all | bytes 2293760 | tf_op jit(solution)/shard_map/all_to_all | solution.py:41
  321.0 3.4 reshape.140
  324.4 2.8 copy.57
  327.3 1.4 copy.58
  328.6 7.7 %reduce-scatter.6.cloned.1.call-done = f32[16,3584]{1,0:T(8,128)} async-done(((f32[128,3584]{1,0:T(8,128)}), f32[16,3584]{1,0:T(8,128)}) %reduce-scatter.6.cloned.1.call-update) | async-done | bytes 229392 | tf_op jit(solution)/shard_map/reduce_scatter | solution.py:81
  336.3 1.6 convert_element_type.53
  337.9 55.1 %all-gather.7.cloned.1.call-done = bf16[256,1,17920]{2,0,1:T(8,128)(2,1)} async-done(((bf16[32,1,17920]{2,0,1:T(8,128)(2,1)}), bf16[256,1,17920]{2,0,1:T(8,128)(2,1)}) %all-gather.7.cloned.1.call-update) | async-done | bytes 9175056 | tf_op jit(solution)/shard_map/all_gather | solution.py:43
  393.0 1.6 slice_dynamic-update-slice_fusion.4
  394.6 1.6 slice_dynamic-update-slice_fusion.3
  396.2 1.6 slice_dynamic-update-slice_fusion.2
  397.8 1.6 slice_dynamic-update-slice_fusion.1
  399.5 1.6 slice_dynamic-update-slice_fusion
  401.1 3.4 fusion.2
  404.5 2.8 fusion.5
  407.4 3.5 fusion.1
  410.9 3.7 fusion
  (66 shorter events, 1.8 us)
Async XLA Ops:
  7.2 133.7 %copy-start = (bf16[1,224,3584]{2,1,0:T(8,128)(2,1)S(1)}, bf16[1,224,3584]{2,1,0:T(8,128)(2,1)}, u32[]{:S(2)}) copy-start(bf16[1,224,3584]{2,1,0:T(8,128)(2,1)} %param.13) | copy-start | bytes 4816900
  7.2 11.1 %copy-start.2 = (bf16[128,3584]{1,0:T(8,128)(2,1)S(1)}, bf16[128,3584]{1,0:T(8,128)(2,1)}, u32[]{:S(2)}) copy-start(bf16[128,3584]{1,0:T(8,128)(2,1)} %param.7) | copy-start | bytes 2752516
  7.2 117.7 %all-gather.5.cloned.1.call-start = ((), (), s32[]{:S(2)}) async-start(), calls=%async_computation.9 | async-start | bytes 10321920 | tf_op jit(solution)/shard_map/all_gather | solution.py:42
  18.9 1.0 copy-start.1
  73.3 136.3 %reduce-scatter.4.cloned.1.call-start = ((), (), s32[]{:S(2)}) async-start(), calls=%async_computation.6 | async-start | bytes 10321920 | tf_op jit(solution)/shard_map/reduce_scatter | solution.py:68
  131.3 2.0 copy-start.6
  133.3 3.6 copy-start.4
  133.3 3.6 copy-start.7
  136.9 3.9 copy-start.8
  213.6 10.6 %copy-start.5 = (f32[128,8]{0,1:T(8,128)S(1)}, f32[128,8]{0,1:T(8,128)}, u32[]{:S(2)}) copy-start(f32[128,8]{0,1:T(8,128)} %param.10) | copy-start | bytes 12292
  213.6 38.1 %all-to-all-start.1 = ((bf16[32,2,8960]{2,1,0:T(2,128)(2,1)}), bf16[32,2,8960]{2,1,0:T(2,128)(2,1)S(1)}, u32[]{:S(2)}, u32[]{:S(2)}) async-start(bf16[32,2,8960]{2,1,0:T(2,128)(2,1)} %reshape.137), calls=%async_computation.2 | async-start | bytes 2293760 | tf_op jit(solution)/shard_map/all_to_all | solution.py:69
  223.9 103.4 %reduce-scatter.8.cloned.1.call-start = ((), (), s32[]{:S(2)}) async-start(), calls=%async_computation.8 | async-start | bytes 73728 | tf_op jit(solution)/shard_map/reduce_scatter | solution.py:82
  256.9 1.2 copy-start.3
  267.3 69.0 %reduce-scatter.6.cloned.1.call-start = ((), (), s32[]{:S(2)}) async-start(), calls=%async_computation.7 | async-start | bytes 2064384 | tf_op jit(solution)/shard_map/reduce_scatter | solution.py:81
  275.4 117.5 %all-gather.7.cloned.1.call-start = ((), (), s32[]{:S(2)}) async-start(), calls=%async_computation.10 | async-start | bytes 10321920 | tf_op jit(solution)/shard_map/all_gather | solution.py:43
  401.1 6.3 %slice-start = ((s8[9175040]{0:T(1024)(128)(4,1)}), s8[4194304]{0:T(1024)(128)(4,1)S(1)}, s32[]{:S(2)}) async-start(s8[9175040]{0:T(1024)(128)(4,1)} %bitcast.72), calls=%async_computation.11 | async-start | bytes 8388608
  401.1 6.3 %slice-start.1 = ((s8[9175040]{0:T(1024)(128)(4,1)}), s8[4194304]{0:T(1024)(128)(4,1)S(1)}, s32[]{:S(2)}) async-start(s8[9175040]{0:T(1024)(128)(4,1)} %bitcast.72), calls=%async_computation.12 | async-start | bytes 8388608
  404.5 2.9 slice-start.2
  404.5 2.9 copy-start.9
  407.4 3.5 copy-start.10
Sparse Core Ops, SparseCore 0:
  73.5 51.3 all-gather.4
  150.6 58.9 reduce-scatter.3
  267.5 31.3 reduce-scatter.7
  301.3 34.9 reduce-scatter.5
  338.6 54.3 all-gather.6

commit v3 on v2

--- a/solution.py
+++ b/solution.py
@@ -37,10 +37,12 @@
             [packed[:, r * width : (r + 1) * width] for r in range(share)], axis=0
         )
 
-    recv_x = lax.all_to_all(to_lanes(send_x), "expert", split_axis=0, concat_axis=0, tiled=True)
-    recv_dy = lax.all_to_all(to_lanes(send_dy), "expert", split_axis=0, concat_axis=0, tiled=True)
-    flat_x = lanes_to_rows(lax.all_gather(recv_x, "dp", axis=0, tiled=True))
-    flat_dy = lanes_to_rows(lax.all_gather(recv_dy, "dp", axis=0, tiled=True))
+    packed = jnp.concatenate([to_lanes(send_x), to_lanes(send_dy)], axis=1)
+    recv = lax.all_to_all(packed, "expert", split_axis=0, concat_axis=0, tiled=True)
+    gathered = lax.all_gather(recv, "dp", axis=0, tiled=True)
+    half = share * width
+    flat_x = lanes_to_rows(gathered[:, :half])
+    flat_dy = lanes_to_rows(gathered[:, half:])
     gate_local = w_gate[0]
     up_local = w_up[0]
     down_local = w_down[0]

time: 424 us -> 431 us (1.017)
  waiting for transfers between devices: 201 us -> 224 us
  blocking collectives: 81 us -> 67.1 us
  matrix products: 27.9 us -> 33.2 us
  local copies, waits for them, and re-layouts: 67.3 us -> 62.1 us
    reduce_scatter x1, waiting for transfers between devices: 7.67 us -> 35.9 us  [body(): lax.psum_scatter(out_part, 'dp', scatter_dimension=0, tiled=True)]
    all_gather x2 -> x1, waiting for transfers between devices: 107 us -> 90.2 us  [body(): gathered = lax.all_gather(recv, 'dp', axis=0, tiled=True)]
    all_to_all x2 -> x1, blocking collectives: 81 us -> 67.1 us  [body(): lax.all_to_all(packed, 'expert', split_axis=0, concat_axis=0, tiled=True)]
    reduce_scatter x1, waiting for transfers between devices: 0.02 us -> 10.6 us  [body(): lax.psum_scatter(grad_part, 'dp', scatter_dimension=0, tiled=True)]
    unnamed x62 -> x63, local copies, waits for them, and re-layouts: 46.3 us -> 44.9 us
  transfers between devices with their start and end apart: 6 -> 5, of which waited for: 5 -> 5; matrix products, arithmetic and copies ran while one was open for 6% -> 5% of each run, Pallas kernels for 0% -> 0%
where the time goes in v3:
time: 431 us; the launch traced here: 430 us
  waiting for transfers between devices  224 us (52%)
  blocking collectives  67.1 us (16%)
  local copies, waits for them, and re-layouts  62.1 us (14%)
  matrix products  33.2 us (8%)
  other arithmetic  19.1 us (4%)
  between operations  14.2 us (3%)
  starting transfers between devices  10.7 us (2%)
    all_gather x1, waiting for transfers between devices, body(): gathered = lax.all_gather(recv, 'dp', axis=0, tiled=True)  90.2 us
    all_to_all x1, blocking collectives, body(): lax.all_to_all(packed, 'expert', split_axis=0, concat_axis=0, tiled=True)  67.1 us
    reduce_scatter x1, waiting for transfers between devices, body(): y_sum = lax.psum_scatter(y_lanes, 'dp', scatter_dimension=0, tiled=True)  59.6 us
    unnamed x63, local copies, waits for them, and re-layouts  44.9 us
    reduce_scatter x1, waiting for transfers between devices, body(): lax.psum_scatter(out_part, 'dp', scatter_dimension=0, tiled=True)  35.9 us
    all_to_all x1, waiting for transfers between devices, body(): lax.all_to_all(y_sum, 'expert', split_axis=0, concat_axis=0, tiled=True)  27.6 us
    reduce_scatter x1, waiting for transfers between devices, body(): lax.psum_scatter(grad_part, 'dp', scatter_dimension=0, tiled=True)  10.6 us
    all_to_all x1, starting transfers between devices, body(): lax.all_to_all(y_sum, 'expert', split_axis=0, concat_axis=0, tiled=True)  10.2 us
  transfers between devices with their start and end apart: 5, of which 5 were waited for; matrix products, arithmetic and copies ran while one was open for 5% of the time, Pallas kernels for 0%

profile of v3, /device:TPU:8, one launch (start us, length us, event | category | flops | bytes accessed | tf_op | source)
XLA Modules:
  0.0 430.4 jit_solution(4019595636521193361)
XLA Ops:
  7.2 0.9 copy.42
  8.1 0.1 eq.45
  8.2 0.1 eq.49
  8.3 0.8 copy.48
  9.1 0.1 mul.85
  9.2 9.0 %reduce-window.6 = s32[32,8,128]{2,1,0:T(8,128)S(1)} reduce-window(s32[32,8,128]{2,1,0:T(8,128)S(1)} %fusion.17, s32[]{:T(128)} %constant.11.clone.1), window={size=1x1x128 pad=0_0x0_0x127_0}, to_apply=%region_0.0 | reduce-window | flops 4161536 | bytes 262148 | tf_op jit(solution)/shard_map/reduce-window
  18.2 0.1 slice.142
  18.3 0.1 copy.44
  18.5 0.1 copy.45
  18.6 0.1 broadcast_add_fusion
  18.8 0.1 and.22
  18.9 0.1 mul.84
  19.0 0.1 convert_reduce_fusion
  19.1 1.7 convolution_convert_fusion.4
  21.0 0.1 select_reduce_fusion
  21.1 1.9 multiply_convert_fusion
  23.1 1.4 copy-done.2
  24.5 0.5 broadcast.164
  25.0 4.8 %reduce = bf16[32,35840]{1,0:T(8,128)(2,1)} reduce(bf16[32,1,35840]{2,0,1:T(8,128)(2,1)} %bitcast.62, bf16[]{:T(256)} %broadcast.164), dimensions={1}, to_apply=%copy.49.reduce_sub_computation | reduce | bytes 4587522 | tf_op jit(solution)/shard_map/all_to_all | solution.py:41
  29.8 4.7 %reshape.132 = bf16[32,2,17920]{2,1,0:T(2,128)(2,1)} reshape(bf16[32,35840]{1,0:T(8,128)(2,1)} %reduce) | data formatting | bytes 4587520
  34.4 67.1 %all_to_all.24 = bf16[32,2,17920]{2,1,0:T(2,128)(2,1)} all-to-all(bf16[32,2,17920]{2,1,0:T(2,128)(2,1)} %reshape.132), channel_id=1, replica_groups=mesh['dp'=8,'expert'=32] {'expert'}, dimensions={0} | all-to-all | bytes 4587520 | tf_op jit(solution)/shard_map/all_to_all | solution.py:41
  101.5 10.5 %reshape.133 = bf16[32,1,35840]{2,1,0:T(2,128)(2,1)} reshape(bf16[32,2,17920]{2,1,0:T(2,128)(2,1)} %all_to_all.24) | data formatting | bytes 4587520
  112.0 4.4 %copy.50 = bf16[32,1,35840]{2,0,1:T(8,128)(2,1)} copy(bf16[32,1,35840]{2,1,0:T(2,128)(2,1)} %reshape.133) | data formatting | bytes 4587520 | tf_op jit(solution)/shard_map/all_to_all | solution.py:41
  116.4 0.2 reduce-scatter.4.cloned.1.call-start
  116.7 90.2 %all-gather.3.cloned.1.call-done = bf16[256,1,35840]{2,0,1:T(8,128)(2,1)} async-done(((bf16[32,1,35840]{2,0,1:T(8,128)(2,1)}), bf16[256,1,35840]{2,0,1:T(8,128)(2,1)}) %all-gather.3.cloned.1.call-update) | async-done | bytes 18350096 | tf_op jit(solution)/shard_map/all_gather | solution.py:42
  206.9 2.3 slice_dynamic-update-slice_fusion.4
  209.2 2.3 slice_dynamic-update-slice_fusion.3
  211.5 2.3 slice_dynamic-update-slice_fusion.2
  213.8 2.3 slice_dynamic-update-slice_fusion.1
  216.1 2.4 slice_dynamic-update-slice_fusion
  218.5 0.1 copy-done.6
  218.6 2.8 fusion.10
  221.4 0.7 copy-done.4
  222.1 2.8 copy-done.5
  224.9 3.9 multiply_convert_fusion.3
  228.8 2.6 convolution_convert_fusion
  231.3 1.4 slice_dynamic-update-slice_fusion.9
  232.8 1.4 slice_dynamic-update-slice_fusion.8
  234.2 1.4 slice_dynamic-update-slice_fusion.7
  235.6 1.4 slice_dynamic-update-slice_fusion.6
  236.9 1.4 slice_dynamic-update-slice_fusion.5
  238.4 59.6 %reduce-scatter.4.cloned.1.call-done = bf16[32,17920]{1,0:T(8,128)(2,1)} async-done(((bf16[256,17920]{1,0:T(8,128)(2,1)}), bf16[32,17920]{1,0:T(8,128)(2,1)}) %reduce-scatter.4.cloned.1.call-update) | async-done | bytes 1146896 | tf_op jit(solution)/shard_map/reduce_scatter | solution.py:70
  298.0 2.8 reduce.1
  300.8 1.2 reshape.134
  301.9 10.2 %all-to-all-start.1 = ((bf16[32,2,8960]{2,1,0:T(2,128)(2,1)}), bf16[32,2,8960]{2,1,0:T(2,128)(2,1)S(1)}, u32[]{:S(2)}, u32[]{:S(2)}) async-start(bf16[32,2,8960]{2,1,0:T(2,128)(2,1)} %reshape.134), calls=%async_computation.2 | async-start | bytes 2293760 | tf_op jit(solution)/shard_map/all_to_all | solution.py:71
  312.1 0.1 reshape.121
  312.3 27.6 %all-to-all-done.1 = bf16[32,2,8960]{2,1,0:T(2,128)(2,1)S(1)} async-done(((bf16[32,2,8960]{2,1,0:T(2,128)(2,1)}), bf16[32,2,8960]{2,1,0:T(2,128)(2,1)S(1)}, u32[]{:S(2)}, u32[]{:S(2)}) %all-to-all-start.1) | async-done | bytes 1146912 | tf_op jit(solution)/shard_map/all_to_all | solution.py:71
  339.8 3.4 reshape.135
  343.3 1.9 copy.58
  345.3 0.3 copy-done.1
  345.6 0.4 fusion.4
  346.0 0.1 pad_maximum_fusion
  346.1 6.8 %gather_fusion = f32[1024]{0:T(1024)S(1)} fusion(f32[161]{0:T(256)S(1)} %pad_maximum_fusion, s32[1024]{0:T(1024)S(1)} %broadcast_clamp_fusion), kind=kCustom, calls=%fused_computation | custom fusion | bytes 12288 | tf_op jit(solution)/shard_map/gather | solution.py:82
  352.9 0.7 reshape.122
  353.6 0.3 reduce-scatter.6.cloned.1.call-start
  353.9 3.1 fusion.3
  357.1 7.2 %fusion.2 = bf16[1,224,3584]{2,1,0:T(8,128)(2,1)} fusion(bf16[1280,224]{0,1:T(8,128)(2,1)S(1)} %get-tuple-element.40, bf16[1280,3584]{1,0:T(8,128)(2,1)} %copy-done.4), kind=kOutput, calls=%fused_computation.8 | convolution fusion | flops 2056011776 | bytes 11354112 | tf_op jit(solution)/shard_map/dot_general | solution.py:63
  364.3 2.8 fusion.5
  367.2 3.5 fusion.1
  370.6 3.7 fusion
  374.4 10.6 %reduce-scatter.8.cloned.1.call-done = f32[16,8]{1,0:T(8,128)} async-done(((f32[128,8]{1,0:T(8,128)}), f32[16,8]{1,0:T(8,128)}) %reduce-scatter.8.cloned.1.call-update) | async-done | bytes 528 | tf_op jit(solution)/shard_map/reduce_scatter | solution.py:84
  385.0 1.4 copy.53
  386.4 35.9 %reduce-scatter.6.cloned.1.call-done = f32[16,3584]{1,0:T(8,128)} async-done(((f32[128,3584]{1,0:T(8,128)}), f32[16,3584]{1,0:T(8,128)}) %reduce-scatter.6.cloned.1.call-update) | async-done | bytes 229392 | tf_op jit(solution)/shard_map/reduce_scatter | solution.py:83
  422.3 1.6 convert_element_type.54
  (61 shorter events, 0.7 us)
Async XLA Ops:
  7.2 221.6 %copy-start = (bf16[1,224,3584]{2,1,0:T(8,128)(2,1)S(1)}, bf16[1,224,3584]{2,1,0:T(8,128)(2,1)}, u32[]{:S(2)}) copy-start(bf16[1,224,3584]{2,1,0:T(8,128)(2,1)} %param.13) | copy-start | bytes 4816900
  7.2 199.7 %all-gather.3.cloned.1.call-start = ((), (), s32[]{:S(2)}) async-start(), calls=%async_computation.8 | async-start | bytes 20643840 | tf_op jit(solution)/shard_map/all_gather | solution.py:42
  19.0 2.1 copy-start.3
  23.1 1.4 copy-start.2
  116.4 181.5 %reduce-scatter.4.cloned.1.call-start = ((), (), s32[]{:S(2)}) async-start(), calls=%async_computation.5 | async-start | bytes 10321920 | tf_op jit(solution)/shard_map/reduce_scatter | solution.py:70
  216.1 2.5 copy-start.6
  218.5 3.6 copy-start.4
  218.5 6.4 %copy-start.5 = (bf16[1280,3584]{1,0:T(8,128)(2,1)}, bf16[1280,3584]{1,0:T(8,128)(2,1)S(1)}, u32[]{:S(2)}) copy-start(bf16[1280,3584]{1,0:T(8,128)(2,1)S(1)} %get-tuple-element.29) | copy-start | bytes 27525124
  218.6 6.3 %copy-start.7 = (bf16[1,224,3584]{2,1,0:T(8,128)(2,1)S(1)}, bf16[1,224,3584]{2,1,0:T(8,128)(2,1)}, u32[]{:S(2)}) copy-start(bf16[1,224,3584]{2,1,0:T(8,128)(2,1)} %param.12) | copy-start | bytes 4816900
  224.9 3.9 copy-start.8
  301.9 37.9 %all-to-all-start.1 = ((bf16[32,2,8960]{2,1,0:T(2,128)(2,1)}), bf16[32,2,8960]{2,1,0:T(2,128)(2,1)S(1)}, u32[]{:S(2)}, u32[]{:S(2)}) async-start(bf16[32,2,8960]{2,1,0:T(2,128)(2,1)} %reshape.134), calls=%async_computation.2 | async-start | bytes 2293760 | tf_op jit(solution)/shard_map/all_to_all | solution.py:71
  312.1 72.9 %reduce-scatter.8.cloned.1.call-start = ((), (), s32[]{:S(2)}) async-start(), calls=%async_computation.7 | async-start | bytes 73728 | tf_op jit(solution)/shard_map/reduce_scatter | solution.py:84
  343.3 2.3 copy-start.1
  353.6 68.6 %reduce-scatter.6.cloned.1.call-start = ((), (), s32[]{:S(2)}) async-start(), calls=%async_computation.6 | async-start | bytes 2064384 | tf_op jit(solution)/shard_map/reduce_scatter | solution.py:83
  357.0 7.2 %slice-start = ((s8[9175040]{0:T(1024)(128)(4,1)}), s8[786432]{0:T(1024)(128)(4,1)S(1)}, s32[]{:S(2)}) async-start(s8[9175040]{0:T(1024)(128)(4,1)} %bitcast.65), calls=%async_computation.9 | async-start | bytes 1572864
  357.0 7.2 %slice-start.1 = ((s8[9175040]{0:T(1024)(128)(4,1)}), s8[4194304]{0:T(1024)(128)(4,1)S(1)}, s32[]{:S(2)}) async-start(s8[9175040]{0:T(1024)(128)(4,1)} %bitcast.65), calls=%async_computation.10 | async-start | bytes 8388608
  357.0 7.2 %slice-start.2 = ((s8[9175040]{0:T(1024)(128)(4,1)}), s8[4194304]{0:T(1024)(128)(4,1)S(1)}, s32[]{:S(2)}) async-start(s8[9175040]{0:T(1024)(128)(4,1)} %bitcast.65), calls=%async_computation.11 | async-start | bytes 8388608
  357.0 10.1 %slice-start.3 = ((s8[9175040]{0:T(1024)(128)(4,1)}), s8[4194304]{0:T(1024)(128)(4,1)S(1)}, s32[]{:S(2)}) async-start(s8[9175040]{0:T(1024)(128)(4,1)} %bitcast.67), calls=%async_computation.12 | async-start | bytes 8388608
  357.1 10.1 %slice-start.4 = ((s8[9175040]{0:T(1024)(128)(4,1)}), s8[4194304]{0:T(1024)(128)(4,1)S(1)}, s32[]{:S(2)}) async-start(s8[9175040]{0:T(1024)(128)(4,1)} %bitcast.67), calls=%async_computation.13 | async-start | bytes 8388608
  364.2 2.9 slice-start.5
  364.2 2.9 copy-start.9
  367.2 3.5 copy-start.10
Sparse Core Ops, SparseCore 0:
  116.6 90.2 all-gather.2
  238.5 59.4 reduce-scatter.3
  353.8 31.2 reduce-scatter.7
  387.5 34.7 reduce-scatter.5

commit v4 on v2

--- a/solution.py
+++ b/solution.py
@@ -38,7 +38,8 @@
         )
 
     recv_x = lax.all_to_all(to_lanes(send_x), "expert", split_axis=0, concat_axis=0, tiled=True)
-    recv_dy = lax.all_to_all(to_lanes(send_dy), "expert", split_axis=0, concat_axis=0, tiled=True)
+    recv_x, lanes_dy = lax.optimization_barrier((recv_x, to_lanes(send_dy)))
+    recv_dy = lax.all_to_all(lanes_dy, "expert", split_axis=0, concat_axis=0, tiled=True)
     flat_x = lanes_to_rows(lax.all_gather(recv_x, "dp", axis=0, tiled=True))
     flat_dy = lanes_to_rows(lax.all_gather(recv_dy, "dp", axis=0, tiled=True))
     gate_local = w_gate[0]
@@ -66,6 +67,9 @@
         [y_part[r * stack_rows : (r + 1) * stack_rows] for r in range(share)], axis=1
     )
     y_sum = lax.psum_scatter(y_lanes, "dp", scatter_dimension=0, tiled=True)
+    y_sum, grad_gate, grad_up, grad_down = lax.optimization_barrier(
+        (y_sum, grad_gate, grad_up, grad_down)
+    )
     y_back = lax.all_to_all(y_sum, "expert", split_axis=0, concat_axis=0, tiled=True)
     y_home = lanes_to_rows(y_back).astype(jnp.float32)
     out_part = lax.dot_general(

time: 424 us -> 379 us (0.89)
  blocking collectives: 81 us -> 38.4 us
  starting transfers between devices: 10.7 us -> 22.4 us
  waiting for transfers between devices: 201 us -> 190 us
  local copies, waits for them, and re-layouts: 67.3 us -> 62.9 us
    all_gather x1, waiting for transfers between devices: 51.5 us -> 5.64 us  [body(): flat_x = lanes_to_rows(lax.all_gather(recv_x, 'dp', axis=0, tiled=True))]
    all_to_all x2 -> x1, blocking collectives: 81 us -> 38.4 us  [body(): lax.all_to_all(lanes_dy, 'expert', split_axis=0, concat_axis=0, tiled=True)]
    reduce_scatter x1, waiting for transfers between devices: 0.02 us -> 28.2 us  [body(): lax.psum_scatter(grad_part, 'dp', scatter_dimension=0, tiled=True)]
    reduce_scatter x1, waiting for transfers between devices: 7.67 us -> 35.8 us  [body(): lax.psum_scatter(out_part, 'dp', scatter_dimension=0, tiled=True)]
    all_gather x1, waiting for transfers between devices: 55.1 us -> 32.1 us  [body(): flat_dy = lanes_to_rows(lax.all_gather(recv_dy, 'dp', axis=0, tiled=True))]
    all_to_all x0 -> x1, waiting for transfers between devices: none -> 21.1 us  [body(): lax.all_to_all(to_lanes(send_x), 'expert', split_axis=0, concat_axis=0, t...]
    reduce_scatter x1, waiting for transfers between devices: 59.1 us -> 39.7 us  [body(): y_sum = lax.psum_scatter(y_lanes, 'dp', scatter_dimension=0, tiled=True)]
    all_to_all x0 -> x1, starting transfers between devices: none -> 11.8 us  [body(): lax.all_to_all(to_lanes(send_x), 'expert', split_axis=0, concat_axis=0, t...]
  transfers between devices with their start and end apart: 6 -> 7, of which waited for: 5 -> 7; matrix products, arithmetic and copies ran while one was open for 6% -> 18% of each run, Pallas kernels for 0% -> 0%
where the time goes in v4:
time: 379 us; the launch traced here: 378 us
  waiting for transfers between devices  190 us (50%)
  local copies, waits for them, and re-layouts  62.9 us (17%)
  blocking collectives  38.4 us (10%)
  matrix products  29.6 us (8%)
  starting transfers between devices  22.4 us (6%)
  other arithmetic  19.9 us (5%)
  between operations  14.2 us (4%)
    unnamed x63, local copies, waits for them, and re-layouts  45.7 us
    reduce_scatter x1, waiting for transfers between devices, body(): y_sum = lax.psum_scatter(y_lanes, 'dp', scatter_dimension=0, tiled=True)  39.7 us
    all_to_all x1, blocking collectives, body(): lax.all_to_all(lanes_dy, 'expert', split_axis=0, concat_axis=0, tiled=True)  38.4 us
    reduce_scatter x1, waiting for transfers between devices, body(): lax.psum_scatter(out_part, 'dp', scatter_dimension=0, tiled=True)  35.8 us
    all_gather x1, waiting for transfers between devices, body(): flat_dy = lanes_to_rows(lax.all_gather(recv_dy, 'dp', axis=0, tiled=True))  32.1 us
    reduce_scatter x1, waiting for transfers between devices, body(): lax.psum_scatter(grad_part, 'dp', scatter_dimension=0, tiled=True)  28.2 us
    all_to_all x1, waiting for transfers between devices, body(): lax.all_to_all(y_sum, 'expert', split_axis=0, concat_axis=0, tiled=True)  27.6 us
    all_to_all x1, waiting for transfers between devices, body(): lax.all_to_all(to_lanes(send_x), 'expert', split_axis=0, concat_axis=0, t...  21.1 us
  transfers between devices with their start and end apart: 7, of which 7 were waited for; matrix products, arithmetic and copies ran while one was open for 18% of the time, Pallas kernels for 0%

profile of v4, /device:TPU:8, one launch (start us, length us, event | category | flops | bytes accessed | tf_op | source)
XLA Modules:
  0.0 377.5 jit_solution(13135497190365375597)
XLA Ops:
  7.2 0.9 copy.44
  8.3 9.0 %reduce-window.6 = s32[32,8,128]{2,1,0:T(8,128)S(1)} reduce-window(s32[32,8,128]{2,1,0:T(8,128)S(1)} %fusion.16, s32[]{:T(128)} %constant.11.clone.1), window={size=1x1x128 pad=0_0x0_0x127_0}, to_apply=%region_0.0 | reduce-window | flops 4161536 | bytes 262148 | tf_op jit(solution)/shard_map/reduce-window
  18.2 0.4 convolution_convert_fusion.1
  18.8 1.0 copy-done.2
  19.8 0.5 broadcast.164
  20.3 2.8 reduce
  23.1 1.2 reshape.134
  24.3 11.8 %all-to-all-start = ((bf16[32,2,8960]{2,1,0:T(2,128)(2,1)}), bf16[32,2,8960]{2,1,0:T(2,128)(2,1)S(1)}, u32[]{:S(2)}, u32[]{:S(2)}) async-start(bf16[32,2,8960]{2,1,0:T(2,128)(2,1)} %reshape.134), calls=%async_computation | async-start | bytes 2293760 | tf_op jit(solution)/shard_map/all_to_all | solution.py:40
  36.5 3.0 multiply_convert_fusion
  39.6 0.7 slice_dynamic-update-slice_fusion.24
  40.3 0.7 slice_dynamic-update-slice_fusion.23
  41.0 0.7 slice_dynamic-update-slice_fusion.22
  41.7 0.7 slice_dynamic-update-slice_fusion.21
  42.4 0.7 slice_dynamic-update-slice_fusion.20
  43.1 21.1 %all-to-all-done = bf16[32,2,8960]{2,1,0:T(2,128)(2,1)S(1)} async-done(((bf16[32,2,8960]{2,1,0:T(2,128)(2,1)}), bf16[32,2,8960]{2,1,0:T(2,128)(2,1)S(1)}, u32[]{:S(2)}, u32[]{:S(2)}) %all-to-all-start) | async-done | bytes 1146912 | tf_op jit(solution)/shard_map/all_to_all | solution.py:40
  64.2 3.4 reshape.135
  67.6 2.8 copy.64
  70.5 2.8 reduce.1
  73.3 1.2 reshape.136
  74.4 38.4 %all_to_all.36 = bf16[32,2,8960]{2,1,0:T(2,128)(2,1)S(1)} all-to-all(bf16[32,2,8960]{2,1,0:T(2,128)(2,1)} %reshape.136), channel_id=1, replica_groups=mesh['dp'=8,'expert'=32] {'expert'}, dimensions={0} | all-to-all | bytes 2293760 | tf_op jit(solution)/shard_map/all_to_all | solution.py:42
  112.8 3.4 reshape.137
  116.3 2.8 copy.53
  119.1 0.2 reduce-scatter.4.cloned.1.call-start
  119.3 5.6 %all-gather.4.cloned.1.call-done = bf16[256,17920]{1,0:T(8,128)(2,1)} async-done(((bf16[32,17920]{1,0:T(8,128)(2,1)}), bf16[256,17920]{1,0:T(8,128)(2,1)}) %all-gather.4.cloned.1.call-update) | async-done | bytes 9175056 | tf_op jit(solution)/shard_map/all_gather | solution.py:43
  125.0 1.6 slice_dynamic-update-slice_fusion.14
  126.6 1.6 slice_dynamic-update-slice_fusion.13
  128.2 1.6 slice_dynamic-update-slice_fusion.12
  129.8 1.6 slice_dynamic-update-slice_fusion.11
  131.5 1.7 slice_dynamic-update-slice_fusion.10
  133.4 2.8 fusion.7
  136.3 0.8 copy-done.4
  137.0 3.9 %multiply_convert_fusion.3 = (bf16[1280,224]{0,1:T(8,128)(2,1)S(1)}, f32[1280,224]{0,1:T(8,128)}) fusion(f32[1280,224]{0,1:T(8,128)S(1)} %fusion.7, bf16[1280,3584]{1,0:T(8,128)(2,1)S(1)} %slice_dynamic-update-slice_fusion.10, bf16[1,224,3584]{2,1,0:T(8,128)(2,1)S(1)} %copy-done.7), kind=kOutput, calls=%fused_computation.37 | convolution fusion | flops 2056929280 | bytes 13647872 | tf_op jit(solution)/shard_map/dot_general | solution.py:51
  140.9 2.6 convolution_convert_fusion
  143.5 1.4 slice_dynamic-update-slice_fusion.9
  144.9 1.4 slice_dynamic-update-slice_fusion.8
  146.3 1.4 slice_dynamic-update-slice_fusion.7
  147.7 1.4 slice_dynamic-update-slice_fusion.6
  149.1 1.4 slice_dynamic-update-slice_fusion.5
  150.5 32.1 %all-gather.6.cloned.1.call-done = bf16[256,1,17920]{2,0,1:T(8,128)(2,1)} async-done(((bf16[32,1,17920]{2,0,1:T(8,128)(2,1)}), bf16[256,1,17920]{2,0,1:T(8,128)(2,1)}) %all-gather.6.cloned.1.call-update) | async-done | bytes 9175056 | tf_op jit(solution)/shard_map/all_gather | solution.py:44
  182.6 1.6 slice_dynamic-update-slice_fusion.4
  184.2 1.6 slice_dynamic-update-slice_fusion.3
  185.8 1.6 slice_dynamic-update-slice_fusion.2
  187.4 1.6 slice_dynamic-update-slice_fusion.1
  189.1 1.6 slice_dynamic-update-slice_fusion
  190.7 3.4 fusion.24
  194.1 2.8 fusion.2
  197.0 3.5 fusion.11
  200.5 4.0 %fusion.10 = bf16[224,3584]{1,0:T(8,128)(2,1)} fusion(bf16[1280,3584]{1,0:T(8,128)(2,1)S(1)} %bitcast.74, f32[1280,224]{0,1:T(8,128)S(1)} %copy-done.9, f32[1280,224]{0,1:T(8,128)S(1)} %fusion.2, f32[1280,224]{0,1:T(8,128)S(1)} %copy-done.10), kind=kOutput, calls=%fused_computation.44 | convolution fusion | flops 2058076160 | bytes 14221312 | tf_op jit(solution)/shard_map/dot_general | solution.py:63
  204.4 39.7 %reduce-scatter.4.cloned.1.call-done = bf16[32,17920]{1,0:T(8,128)(2,1)} async-done(((bf16[256,17920]{1,0:T(8,128)(2,1)}), bf16[32,17920]{1,0:T(8,128)(2,1)}) %reduce-scatter.4.cloned.1.call-update) | async-done | bytes 1146896 | tf_op jit(solution)/shard_map/reduce_scatter | solution.py:69
  244.1 2.8 reduce.2
  246.9 1.2 reshape.138
  248.1 10.2 %all-to-all-start.2 = ((bf16[32,2,8960]{2,1,0:T(2,128)(2,1)}), bf16[32,2,8960]{2,1,0:T(2,128)(2,1)S(1)}, u32[]{:S(2)}, u32[]{:S(2)}) async-start(bf16[32,2,8960]{2,1,0:T(2,128)(2,1)} %reshape.138), calls=%async_computation.3 | async-start | bytes 2293760 | tf_op jit(solution)/shard_map/all_to_all | solution.py:73
  258.4 27.6 %all-to-all-done.2 = bf16[32,2,8960]{2,1,0:T(2,128)(2,1)S(1)} async-done(((bf16[32,2,8960]{2,1,0:T(2,128)(2,1)}), bf16[32,2,8960]{2,1,0:T(2,128)(2,1)S(1)}, u32[]{:S(2)}, u32[]{:S(2)}) %all-to-all-start.2) | async-done | bytes 1146912 | tf_op jit(solution)/shard_map/all_to_all | solution.py:73
  286.0 3.4 reshape.139
  289.5 1.8 copy.63
  291.4 1.5 copy-done.1
  292.9 0.4 fusion.1
  293.3 6.8 %gather_fusion = f32[1024]{0:T(1024)S(1)} fusion(f32[161]{0:T(256)S(1)} %pad_maximum_fusion, s32[1024]{0:T(1024)S(1)} %broadcast_clamp_fusion), kind=kCustom, calls=%fused_computation | custom fusion | bytes 12288 | tf_op jit(solution)/shard_map/gather | solution.py:84
  300.2 0.7 reshape.124
  300.9 3.1 fusion
  304.1 28.2 %reduce-scatter.8.cloned.1.call-done = f32[16,8]{1,0:T(8,128)} async-done(((f32[128,8]{1,0:T(8,128)}), f32[16,8]{1,0:T(8,128)}) %reduce-scatter.8.cloned.1.call-update) | async-done | bytes 528 | tf_op jit(solution)/shard_map/reduce_scatter | solution.py:86
  332.2 1.4 copy.56
  333.6 35.8 %reduce-scatter.6.cloned.1.call-done = f32[16,3584]{1,0:T(8,128)} async-done(((f32[128,3584]{1,0:T(8,128)}), f32[16,3584]{1,0:T(8,128)}) %reduce-scatter.6.cloned.1.call-update) | async-done | bytes 229392 | tf_op jit(solution)/shard_map/reduce_scatter | solution.py:85
  369.4 1.6 convert_element_type.56
  (68 shorter events, 2.2 us)
Async XLA Ops:
  7.2 133.8 %copy-start = (bf16[1,224,3584]{2,1,0:T(8,128)(2,1)S(1)}, bf16[1,224,3584]{2,1,0:T(8,128)(2,1)}, u32[]{:S(2)}) copy-start(bf16[1,224,3584]{2,1,0:T(8,128)(2,1)} %param.13) | copy-start | bytes 4816900
  7.2 11.1 %copy-start.3 = (bf16[128,3584]{1,0:T(8,128)(2,1)S(1)}, bf16[128,3584]{1,0:T(8,128)(2,1)}, u32[]{:S(2)}) copy-start(bf16[128,3584]{1,0:T(8,128)(2,1)} %param.7) | copy-start | bytes 2752516
  18.8 1.0 copy-start.2
  24.3 11.9 %copy-start.5 = (f32[128,8]{0,1:T(8,128)S(1)}, f32[128,8]{0,1:T(8,128)}, u32[]{:S(2)}) copy-start(f32[128,8]{0,1:T(8,128)} %param.10) | copy-start | bytes 12292
  24.3 40.0 %all-to-all-start = ((bf16[32,2,8960]{2,1,0:T(2,128)(2,1)}), bf16[32,2,8960]{2,1,0:T(2,128)(2,1)S(1)}, u32[]{:S(2)}, u32[]{:S(2)}) async-start(bf16[32,2,8960]{2,1,0:T(2,128)(2,1)} %reshape.134), calls=%async_computation | async-start | bytes 2293760 | tf_op jit(solution)/shard_map/all_to_all | solution.py:40
  36.1 88.9 %all-gather.4.cloned.1.call-start = ((), (), s32[]{:S(2)}) async-start(), calls=%async_computation.6 | async-start | bytes 10321920 | tf_op jit(solution)/shard_map/all_gather | solution.py:43
  70.4 112.1 %all-gather.6.cloned.1.call-start = ((), (), s32[]{:S(2)}) async-start(), calls=%async_computation.10 | async-start | bytes 10321920 | tf_op jit(solution)/shard_map/all_gather | solution.py:44
  119.1 125.1 %reduce-scatter.4.cloned.1.call-start = ((), (), s32[]{:S(2)}) async-start(), calls=%async_computation.7 | async-start | bytes 10321920 | tf_op jit(solution)/shard_map/reduce_scatter | solution.py:69
  131.4 2.0 copy-start.6
  133.4 3.6 copy-start.4
  133.4 3.6 copy-start.7
  137.0 3.9 %copy-start.8 = (f32[1280,224]{0,1:T(8,128)}, f32[1280,224]{0,1:T(8,128)S(1)}, u32[]{:S(2)}) copy-start(f32[1280,224]{0,1:T(8,128)S(1)} %fusion.7) | copy-start | bytes 3440644
  190.7 6.3 %slice-start = ((s8[9175040]{0:T(1024)(128)(4,1)}), s8[4194304]{0:T(1024)(128)(4,1)S(1)}, s32[]{:S(2)}) async-start(s8[9175040]{0:T(1024)(128)(4,1)} %bitcast.73), calls=%async_computation.11 | async-start | bytes 8388608
  190.7 6.3 %slice-start.1 = ((s8[9175040]{0:T(1024)(128)(4,1)}), s8[4194304]{0:T(1024)(128)(4,1)S(1)}, s32[]{:S(2)}) async-start(s8[9175040]{0:T(1024)(128)(4,1)} %bitcast.73), calls=%async_computation.12 | async-start | bytes 8388608
  194.1 2.9 slice-start.2
  194.1 2.9 copy-start.9
  197.0 3.5 copy-start.10
  248.1 38.0 %all-to-all-start.2 = ((bf16[32,2,8960]{2,1,0:T(2,128)(2,1)}), bf16[32,2,8960]{2,1,0:T(2,128)(2,1)S(1)}, u32[]{:S(2)}, u32[]{:S(2)}) async-start(bf16[32,2,8960]{2,1,0:T(2,128)(2,1)} %reshape.138), calls=%async_computation.3 | async-start | bytes 2293760 | tf_op jit(solution)/shard_map/all_to_all | solution.py:73
  258.2 74.0 %reduce-scatter.8.cloned.1.call-start = ((), (), s32[]{:S(2)}) async-start(), calls=%async_computation.9 | async-start | bytes 73728 | tf_op jit(solution)/shard_map/reduce_scatter | solution.py:86
  291.2 1.6 copy-start.1
  300.9 68.5 %reduce-scatter.6.cloned.1.call-start = ((), (), s32[]{:S(2)}) async-start(), calls=%async_computation.8 | async-start | bytes 2064384 | tf_op jit(solution)/shard_map/reduce_scatter | solution.py:85
Sparse Core Ops, SparseCore 0:
  70.6 54.3 all-gather.3
  126.8 55.7 all-gather.5
  185.1 58.9 reduce-scatter.3
  301.0 31.1 reduce-scatter.7
  334.7 34.6 reduce-scatter.5

commit v5 on v4

--- a/solution.py
+++ b/solution.py
@@ -15,7 +15,12 @@
     n_dest = groups * share
     flat_ids = route_ids.reshape(-1)
     onehot = (flat_ids[:, None] == jnp.arange(groups, dtype=jnp.int32)[None, :]).astype(jnp.int32)
-    slot_rank = jnp.sum(jnp.cumsum(onehot, axis=0) * onehot, axis=1) - 1
+    n_slots = flat_ids.shape[0]
+    lower = (
+        jnp.arange(n_slots, dtype=jnp.int32)[:, None] >= jnp.arange(n_slots, dtype=jnp.int32)[None, :]
+    ).astype(jnp.bfloat16)
+    running = jnp.dot(lower, onehot.astype(jnp.bfloat16), preferred_element_type=jnp.float32)
+    slot_rank = jnp.sum(running.astype(jnp.int32) * onehot, axis=1) - 1
     local_rank = slot_rank - dp_idx * share
     mine = (local_rank >= 0) & (local_rank < share)
     dest = jnp.where(mine, local_rank * groups + flat_ids, n_dest)
@@ -82,8 +87,11 @@
     dot_dest = jnp.sum(cot_sel * y_home, axis=1)
     dot_ext = jnp.concatenate([dot_dest, jnp.zeros((1,), jnp.float32)])
     grad_part = dot_ext[dest].reshape(tok_rows, top_slots)
-    layer_sum = lax.psum_scatter(out_part, "dp", scatter_dimension=0, tiled=True)
-    gate_sum = lax.psum_scatter(grad_part, "dp", scatter_dimension=0, tiled=True)
+    both_sum = lax.psum_scatter(
+        jnp.concatenate([out_part, grad_part], axis=1), "dp", scatter_dimension=0, tiled=True
+    )
+    layer_sum = both_sum[:, :width]
+    gate_sum = both_sum[:, width:]
     return (
         layer_sum.astype(jnp.bfloat16),
         gate_sum,

time: 379 us -> 338 us (0.89)
  waiting for transfers between devices: 190 us -> 161 us
  other arithmetic: 19.9 us -> 10.4 us
    reduce_scatter x2 -> x1, waiting for transfers between devices: 63.9 us -> 34.2 us  [body(): lax.psum_scatter(jnp.concatenate([out_part, grad_part], axis=1), 'dp', sc...]
    another operation x3 -> x0, other arithmetic: 9.15 us -> none
    unnamed x63 -> x59, local copies, waits for them, and re-layouts: 45.7 us -> 43.5 us
  transfers between devices with their start and end apart: 7 -> 6, of which waited for: 7 -> 6; matrix products, arithmetic and copies ran while one was open for 18% -> 19% of each run, Pallas kernels for 0% -> 0%
where the time goes in v5:
time: 338 us; the launch traced here: 337 us
  waiting for transfers between devices  161 us (48%)
  local copies, waits for them, and re-layouts  62 us (18%)
  blocking collectives  38.4 us (11%)
  matrix products  29 us (9%)
  starting transfers between devices  22.3 us (7%)
  between operations  14.2 us (4%)
  other arithmetic  10.4 us (3%)
    unnamed x59, local copies, waits for them, and re-layouts  43.5 us
    reduce_scatter x1, waiting for transfers between devices, body(): y_sum = lax.psum_scatter(y_lanes, 'dp', scatter_dimension=0, tiled=True)  39.6 us
    all_to_all x1, blocking collectives, body(): lax.all_to_all(lanes_dy, 'expert', split_axis=0, concat_axis=0, tiled=True)  38.4 us
    reduce_scatter x1, waiting for transfers between devices, body(): lax.psum_scatter(jnp.concatenate([out_part, grad_part], axis=1), 'dp', sc...  34.2 us
    all_gather x1, waiting for transfers between devices, body(): flat_dy = lanes_to_rows(lax.all_gather(recv_dy, 'dp', axis=0, tiled=True))  32.6 us
    all_to_all x1, waiting for transfers between devices, body(): lax.all_to_all(y_sum, 'expert', split_axis=0, concat_axis=0, tiled=True)  27.6 us
    all_to_all x1, waiting for transfers between devices, body(): lax.all_to_all(to_lanes(send_x), 'expert', split_axis=0, concat_axis=0, t...  21.1 us
    all_to_all x1, starting transfers between devices, body(): lax.all_to_all(to_lanes(send_x), 'expert', split_axis=0, concat_axis=0, t...  11.8 us
  transfers between devices with their start and end apart: 6, of which 6 were waited for; matrix products, arithmetic and copies ran while one was open for 19% of the time, Pallas kernels for 0%

profile of v5, /device:TPU:8, one launch (start us, length us, event | category | flops | bytes accessed | tf_op | source)
XLA Modules:
  0.0 337.2 jit_solution(6550261482936504527)
XLA Ops:
  7.2 0.9 copy.36
  8.2 0.5 fusion.13
  9.2 0.4 convolution_convert_fusion.1
  9.8 1.0 copy-done.2
  10.7 0.5 broadcast.151
  11.3 2.8 reduce
  14.0 1.2 reshape.117
  15.2 11.8 %all-to-all-start = ((bf16[32,2,8960]{2,1,0:T(2,128)(2,1)}), bf16[32,2,8960]{2,1,0:T(2,128)(2,1)S(1)}, u32[]{:S(2)}, u32[]{:S(2)}) async-start(bf16[32,2,8960]{2,1,0:T(2,128)(2,1)} %reshape.117), calls=%async_computation | async-start | bytes 2293760 | tf_op jit(solution)/shard_map/all_to_all | solution.py:45
  27.4 3.1 multiply_convert_fusion
  30.5 0.7 slice_dynamic-update-slice_fusion.24
  31.2 0.7 slice_dynamic-update-slice_fusion.23
  31.9 0.7 slice_dynamic-update-slice_fusion.22
  32.6 0.7 slice_dynamic-update-slice_fusion.21
  33.3 0.7 slice_dynamic-update-slice_fusion.20
  34.0 21.1 %all-to-all-done = bf16[32,2,8960]{2,1,0:T(2,128)(2,1)S(1)} async-done(((bf16[32,2,8960]{2,1,0:T(2,128)(2,1)}), bf16[32,2,8960]{2,1,0:T(2,128)(2,1)S(1)}, u32[]{:S(2)}, u32[]{:S(2)}) %all-to-all-start) | async-done | bytes 1146912 | tf_op jit(solution)/shard_map/all_to_all | solution.py:45
  55.2 3.4 %reshape.118 = bf16[32,1,17920]{2,1,0:T(2,128)(2,1)} reshape(bf16[32,2,8960]{2,1,0:T(2,128)(2,1)S(1)} %all-to-all-done) | data formatting | bytes 2293760
  58.6 2.8 copy.51
  61.4 2.8 reduce.1
  64.2 1.2 reshape.119
  65.4 38.4 %all_to_all.36 = bf16[32,2,8960]{2,1,0:T(2,128)(2,1)S(1)} all-to-all(bf16[32,2,8960]{2,1,0:T(2,128)(2,1)} %reshape.119), channel_id=1, replica_groups=mesh['dp'=8,'expert'=32] {'expert'}, dimensions={0} | all-to-all | bytes 2293760 | tf_op jit(solution)/shard_map/all_to_all | solution.py:47
  103.8 3.4 %reshape.120 = bf16[32,1,17920]{2,1,0:T(2,128)(2,1)} reshape(bf16[32,2,8960]{2,1,0:T(2,128)(2,1)S(1)} %all_to_all.36) | data formatting | bytes 2293760
  107.2 2.8 copy.42
  110.0 0.2 reduce-scatter.3.cloned.1.call-start
  110.2 5.7 %all-gather.4.cloned.1.call-done = bf16[256,17920]{1,0:T(8,128)(2,1)} async-done(((bf16[32,17920]{1,0:T(8,128)(2,1)}), bf16[256,17920]{1,0:T(8,128)(2,1)}) %all-gather.4.cloned.1.call-update) | async-done | bytes 9175056 | tf_op jit(solution)/shard_map/all_gather | solution.py:48
  115.9 1.6 slice_dynamic-update-slice_fusion.14
  117.5 1.6 slice_dynamic-update-slice_fusion.13
  119.1 1.6 slice_dynamic-update-slice_fusion.12
  120.8 1.6 slice_dynamic-update-slice_fusion.11
  122.4 1.7 slice_dynamic-update-slice_fusion.10
  124.1 0.2 copy-done.6
  124.4 2.8 fusion.8
  127.2 0.8 copy-done.4
  128.0 3.9 %multiply_convert_fusion.3 = (bf16[1280,224]{0,1:T(8,128)(2,1)S(1)}, f32[1280,224]{0,1:T(8,128)}) fusion(f32[1280,224]{0,1:T(8,128)S(1)} %fusion.8, bf16[1280,3584]{1,0:T(8,128)(2,1)S(1)} %slice_dynamic-update-slice_fusion.10, bf16[1,224,3584]{2,1,0:T(8,128)(2,1)S(1)} %copy-done.7), kind=kOutput, calls=%fused_computation.40 | convolution fusion | flops 2056929280 | bytes 13647872 | tf_op jit(solution)/shard_map/dot_general | solution.py:56
  131.8 2.6 convolution_convert_fusion
  134.4 1.4 slice_dynamic-update-slice_fusion.9
  135.8 1.4 slice_dynamic-update-slice_fusion.8
  137.2 1.4 slice_dynamic-update-slice_fusion.7
  138.6 1.4 slice_dynamic-update-slice_fusion.6
  140.0 1.4 slice_dynamic-update-slice_fusion.5
  141.4 32.6 %all-gather.6.cloned.1.call-done = bf16[256,1,17920]{2,0,1:T(8,128)(2,1)} async-done(((bf16[32,1,17920]{2,0,1:T(8,128)(2,1)}), bf16[256,1,17920]{2,0,1:T(8,128)(2,1)}) %all-gather.6.cloned.1.call-update) | async-done | bytes 9175056 | tf_op jit(solution)/shard_map/all_gather | solution.py:49
  174.1 1.6 slice_dynamic-update-slice_fusion.4
  175.7 1.6 slice_dynamic-update-slice_fusion.3
  177.3 1.6 slice_dynamic-update-slice_fusion.2
  178.9 1.6 slice_dynamic-update-slice_fusion.1
  180.6 1.6 slice_dynamic-update-slice_fusion
  182.2 3.4 %fusion.26 = bf16[224,3584]{1,0:T(8,128)(2,1)} fusion(bf16[1280,224]{0,1:T(8,128)(2,1)S(1)} %get-tuple-element.47, bf16[1280,3584]{1,0:T(8,128)(2,1)S(1)} %slice_dynamic-update-slice_fusion), kind=kOutput, calls=%fused_computation.87 | convolution fusion | flops 2055208960 | bytes 11354112 | tf_op jit(solution)/shard_map/dot_general | solution.py:67
  185.6 2.8 fusion.3
  188.5 3.5 %fusion.15 = bf16[224,3584]{1,0:T(8,128)(2,1)} fusion(bf16[1280,3584]{1,0:T(8,128)(2,1)S(1)} %bitcast.59, f32[1280,224]{0,1:T(8,128)S(1)} %fusion.3, f32[1280,224]{0,1:T(8,128)S(1)} %fusion.8), kind=kOutput, calls=%fused_computation.51 | convolution fusion | flops 2056929280 | bytes 13074432 | tf_op jit(solution)/shard_map/dot_general | solution.py:69
  192.0 4.0 %fusion.14 = bf16[224,3584]{1,0:T(8,128)(2,1)} fusion(bf16[1280,3584]{1,0:T(8,128)(2,1)S(1)} %bitcast.59, f32[1280,224]{0,1:T(8,128)S(1)} %fusion.8, f32[1280,224]{0,1:T(8,128)S(1)} %fusion.3, f32[1280,224]{0,1:T(8,128)S(1)} %copy-done.8), kind=kOutput, calls=%fused_computation.50 | convolution fusion | flops 2058076160 | bytes 14221312 | tf_op jit(solution)/shard_map/dot_general | solution.py:68
  196.0 39.6 %reduce-scatter.3.cloned.1.call-done = bf16[32,17920]{1,0:T(8,128)(2,1)} async-done(((bf16[256,17920]{1,0:T(8,128)(2,1)}), bf16[32,17920]{1,0:T(8,128)(2,1)}) %reduce-scatter.3.cloned.1.call-update) | async-done | bytes 1146896 | tf_op jit(solution)/shard_map/reduce_scatter | solution.py:74
  235.7 2.8 reduce.2
  238.4 1.2 reshape.121
  239.6 10.2 %all-to-all-start.2 = ((bf16[32,2,8960]{2,1,0:T(2,128)(2,1)}), bf16[32,2,8960]{2,1,0:T(2,128)(2,1)S(1)}, u32[]{:S(2)}, u32[]{:S(2)}) async-start(bf16[32,2,8960]{2,1,0:T(2,128)(2,1)} %reshape.121), calls=%async_computation.3 | async-start | bytes 2293760 | tf_op jit(solution)/shard_map/all_to_all | solution.py:78
  249.9 27.6 %all-to-all-done.2 = bf16[32,2,8960]{2,1,0:T(2,128)(2,1)S(1)} async-done(((bf16[32,2,8960]{2,1,0:T(2,128)(2,1)}), bf16[32,2,8960]{2,1,0:T(2,128)(2,1)S(1)}, u32[]{:S(2)}, u32[]{:S(2)}) %all-to-all-start.2) | async-done | bytes 1146912 | tf_op jit(solution)/shard_map/all_to_all | solution.py:78
  277.5 3.4 %reshape.122 = bf16[32,1,17920]{2,1,0:T(2,128)(2,1)} reshape(bf16[32,2,8960]{2,1,0:T(2,128)(2,1)S(1)} %all-to-all-done.2) | data formatting | bytes 2293760
  281.0 1.8 copy.50
  282.9 1.9 fusion.1
  284.8 0.3 fusion.2
  285.2 6.8 %gather_fusion = f32[1024]{0:T(1024)S(1)} fusion(f32[161]{0:T(256)S(1)} %pad_maximum_fusion.1, s32[1024]{0:T(1024)S(1)} %broadcast_clamp_fusion), kind=kCustom, calls=%fused_computation | custom fusion | bytes 12288 | tf_op jit(solution)/shard_map/gather | solution.py:89
  292.1 1.4 pad_maximum_fusion
  293.5 34.2 %reduce-scatter.5.cloned.1.call-done = f32[16,3592]{1,0:T(8,128)} async-done(((f32[128,3592]{1,0:T(8,128)}), f32[16,3592]{1,0:T(8,128)}) %reduce-scatter.5.cloned.1.call-update) | async-done | bytes 229904 | tf_op jit(solution)/shard_map/reduce_scatter | solution.py:90
  327.7 0.7 slice.162
  328.4 0.7 copy.45
  329.1 1.6 slice.194
  (54 shorter events, 1.5 us)
Async XLA Ops:
  7.2 124.7 %copy-start = (bf16[1,224,3584]{2,1,0:T(8,128)(2,1)S(1)}, bf16[1,224,3584]{2,1,0:T(8,128)(2,1)}, u32[]{:S(2)}) copy-start(bf16[1,224,3584]{2,1,0:T(8,128)(2,1)} %param.13) | copy-start | bytes 4816900
  7.2 2.0 copy-start.3
  9.7 1.0 copy-start.2
  15.2 11.9 %copy-start.5 = (f32[128,8]{0,1:T(8,128)S(1)}, f32[128,8]{0,1:T(8,128)}, u32[]{:S(2)}) copy-start(f32[128,8]{0,1:T(8,128)} %param.10) | copy-start | bytes 12292
  15.2 40.0 %all-to-all-start = ((bf16[32,2,8960]{2,1,0:T(2,128)(2,1)}), bf16[32,2,8960]{2,1,0:T(2,128)(2,1)S(1)}, u32[]{:S(2)}, u32[]{:S(2)}) async-start(bf16[32,2,8960]{2,1,0:T(2,128)(2,1)} %reshape.117), calls=%async_computation | async-start | bytes 2293760 | tf_op jit(solution)/shard_map/all_to_all | solution.py:45
  27.0 88.9 %all-gather.4.cloned.1.call-start = ((), (), s32[]{:S(2)}) async-start(), calls=%async_computation.5 | async-start | bytes 10321920 | tf_op jit(solution)/shard_map/all_gather | solution.py:48
  61.4 112.7 %all-gather.6.cloned.1.call-start = ((), (), s32[]{:S(2)}) async-start(), calls=%async_computation.8 | async-start | bytes 10321920 | tf_op jit(solution)/shard_map/all_gather | solution.py:49
  110.0 125.6 %reduce-scatter.3.cloned.1.call-start = ((), (), s32[]{:S(2)}) async-start(), calls=%async_computation.6 | async-start | bytes 10321920 | tf_op jit(solution)/shard_map/reduce_scatter | solution.py:74
  122.4 2.0 copy-start.6
  124.4 3.6 %copy-start.4 = (bf16[1280,3584]{1,0:T(8,128)(2,1)}, bf16[1280,3584]{1,0:T(8,128)(2,1)S(1)}, u32[]{:S(2)}) copy-start(bf16[1280,3584]{1,0:T(8,128)(2,1)S(1)} %slice_dynamic-update-slice_fusion.10) | copy-start | bytes 27525124
  124.4 3.6 %copy-start.7 = (bf16[1,224,3584]{2,1,0:T(8,128)(2,1)S(1)}, bf16[1,224,3584]{2,1,0:T(8,128)(2,1)}, u32[]{:S(2)}) copy-start(bf16[1,224,3584]{2,1,0:T(8,128)(2,1)} %param.12) | copy-start | bytes 4816900
  182.2 6.3 %slice-start = ((s8[9175040]{0:T(1024)(128)(4,1)}), s8[4194304]{0:T(1024)(128)(4,1)S(1)}, s32[]{:S(2)}) async-start(s8[9175040]{0:T(1024)(128)(4,1)} %bitcast.58), calls=%async_computation.9 | async-start | bytes 8388608
  182.2 6.3 %slice-start.1 = ((s8[9175040]{0:T(1024)(128)(4,1)}), s8[4194304]{0:T(1024)(128)(4,1)S(1)}, s32[]{:S(2)}) async-start(s8[9175040]{0:T(1024)(128)(4,1)} %bitcast.58), calls=%async_computation.10 | async-start | bytes 8388608
  185.6 2.9 slice-start.2
  188.5 3.6 %copy-start.8 = (f32[1280,224]{0,1:T(8,128)S(1)}, f32[1280,224]{0,1:T(8,128)}, u32[]{:S(2)}) copy-start(f32[1280,224]{0,1:T(8,128)} %get-tuple-element.48) | copy-start | bytes 3440644
  239.6 37.9 %all-to-all-start.2 = ((bf16[32,2,8960]{2,1,0:T(2,128)(2,1)}), bf16[32,2,8960]{2,1,0:T(2,128)(2,1)S(1)}, u32[]{:S(2)}, u32[]{:S(2)}) async-start(bf16[32,2,8960]{2,1,0:T(2,128)(2,1)} %reshape.121), calls=%async_computation.3 | async-start | bytes 2293760 | tf_op jit(solution)/shard_map/all_to_all | solution.py:78
  249.8 77.9 %reduce-scatter.5.cloned.1.call-start = ((), (), s32[]{:S(2)}) async-start(), calls=%async_computation.7 | async-start | bytes 2138112 | tf_op jit(solution)/shard_map/reduce_scatter | solution.py:90
  282.9 1.9 copy-start.1
Sparse Core Ops, SparseCore 0:
  61.5 54.3 all-gather.3
  118.3 55.7 all-gather.5
  176.6 58.9 reduce-scatter.2
  293.6 34.0 reduce-scatter.4

commit v6 on v5

--- a/solution.py
+++ b/solution.py
@@ -46,7 +46,6 @@
     recv_x, lanes_dy = lax.optimization_barrier((recv_x, to_lanes(send_dy)))
     recv_dy = lax.all_to_all(lanes_dy, "expert", split_axis=0, concat_axis=0, tiled=True)
     flat_x = lanes_to_rows(lax.all_gather(recv_x, "dp", axis=0, tiled=True))
-    flat_dy = lanes_to_rows(lax.all_gather(recv_dy, "dp", axis=0, tiled=True))
     gate_local = w_gate[0]
     up_local = w_up[0]
     down_local = w_down[0]
@@ -57,6 +56,16 @@
     sigma_gate = jax.nn.sigmoid(gate_pre)
     hidden = (gate_pre * sigma_gate * up_pre).astype(jnp.bfloat16)
     y_part = jnp.dot(hidden, down_local, preferred_element_type=jnp.float32).astype(jnp.bfloat16)
+    stack_rows = dp_count * groups
+    y_lanes = jnp.concatenate(
+        [y_part[r * stack_rows : (r + 1) * stack_rows] for r in range(share)], axis=1
+    )
+    y_sum = lax.psum_scatter(y_lanes, "dp", scatter_dimension=0, tiled=True)
+    y_sum, recv_dy = lax.optimization_barrier((y_sum, recv_dy))
+    flat_dy = lanes_to_rows(lax.all_gather(recv_dy, "dp", axis=0, tiled=True))
+    y_back = lax.all_to_all(y_sum, "expert", split_axis=0, concat_axis=0, tiled=True)
+    y_back, flat_dy = lax.optimization_barrier((y_back, flat_dy))
+    y_home = lanes_to_rows(y_back).astype(jnp.float32)
     hidden_grad = lax.dot_general(
         flat_dy, down_local, by_feature, preferred_element_type=jnp.float32
     )
@@ -67,16 +76,6 @@
     grad_down = lax.dot_general(hidden, flat_dy, by_row, preferred_element_type=jnp.float32)
     grad_gate = lax.dot_general(grad_gate_pre, flat_x, by_row, preferred_element_type=jnp.float32)
     grad_up = lax.dot_general(grad_up_pre, flat_x, by_row, preferred_element_type=jnp.float32)
-    stack_rows = dp_count * groups
-    y_lanes = jnp.concatenate(
-        [y_part[r * stack_rows : (r + 1) * stack_rows] for r in range(share)], axis=1
-    )
-    y_sum = lax.psum_scatter(y_lanes, "dp", scatter_dimension=0, tiled=True)
-    y_sum, grad_gate, grad_up, grad_down = lax.optimization_barrier(
-        (y_sum, grad_gate, grad_up, grad_down)
-    )
-    y_back = lax.all_to_all(y_sum, "expert", split_axis=0, concat_axis=0, tiled=True)
-    y_home = lanes_to_rows(y_back).astype(jnp.float32)
     out_part = lax.dot_general(
         pick,
         gate_sel[:, None] * y_home,
@@ -85,8 +84,7 @@
         preferred_element_type=jnp.float32,
     )
     dot_dest = jnp.sum(cot_sel * y_home, axis=1)
-    dot_ext = jnp.concatenate([dot_dest, jnp.zeros((1,), jnp.float32)])
-    grad_part = dot_ext[dest].reshape(tok_rows, top_slots)
+    grad_part = jnp.sum(dest_hot * dot_dest[None, :], axis=1).reshape(tok_rows, top_slots)
     both_sum = lax.psum_scatter(
         jnp.concatenate([out_part, grad_part], axis=1), "dp", scatter_dimension=0, tiled=True
     )

time: 338 us -> 320 us (0.947)
  waiting for transfers between devices: 161 us -> 108 us
  blocking collectives: 38.4 us -> 82.4 us
  starting transfers between devices: 22.3 us -> 12.2 us
    all_gather x1, waiting for transfers between devices: 5.65 us -> 54.5 us  [body(): flat_x = lanes_to_rows(lax.all_gather(recv_x, 'dp', axis=0, tiled=True))]
    all_to_all x0 -> x1, blocking collectives: none -> 40.9 us  [body(): lax.all_to_all(y_sum, 'expert', split_axis=0, concat_axis=0, tiled=True)]
    reduce_scatter x1, waiting for transfers between devices: 39.6 us -> 7.26 us  [body(): y_sum = lax.psum_scatter(y_lanes, 'dp', scatter_dimension=0, tiled=True)]
    all_to_all x1 -> x0, waiting for transfers between devices: 27.6 us -> none  [body(): lax.all_to_all(y_sum, 'expert', split_axis=0, concat_axis=0, tiled=True)]
    all_gather x1, waiting for transfers between devices: 32.6 us -> 6.76 us  [body(): flat_dy = lanes_to_rows(lax.all_gather(recv_dy, 'dp', axis=0, tiled=True))]
    reduce_scatter x1, waiting for transfers between devices: 34.2 us -> 18.1 us  [body(): lax.psum_scatter(jnp.concatenate([out_part, grad_part], axis=1), 'dp', sc...]
    all_to_all x1 -> x0, starting transfers between devices: 10.2 us -> none  [body(): lax.all_to_all(y_sum, 'expert', split_axis=0, concat_axis=0, tiled=True)]
    unnamed x59 -> x72, local copies, waits for them, and re-layouts: 43.5 us -> 51.1 us
  transfers between devices with their start and end apart: 6 -> 5, of which waited for: 6 -> 5; matrix products, arithmetic and copies ran while one was open for 19% -> 14% of each run, Pallas kernels for 0% -> 0%
where the time goes in v6:
time: 320 us; the launch traced here: 319 us
  waiting for transfers between devices  108 us (34%)
  blocking collectives  82.4 us (26%)
  local copies, waits for them, and re-layouts  59.9 us (19%)
  matrix products  32.3 us (10%)
  between operations  14.1 us (4%)
  starting transfers between devices  12.2 us (4%)
  other arithmetic  10.5 us (3%)
    all_gather x1, waiting for transfers between devices, body(): flat_x = lanes_to_rows(lax.all_gather(recv_x, 'dp', axis=0, tiled=True))  54.5 us
    unnamed x72, local copies, waits for them, and re-layouts  51.1 us
    all_to_all x1, blocking collectives, body(): lax.all_to_all(lanes_dy, 'expert', split_axis=0, concat_axis=0, tiled=True)  41.6 us
    all_to_all x1, blocking collectives, body(): lax.all_to_all(y_sum, 'expert', split_axis=0, concat_axis=0, tiled=True)  40.9 us
    all_to_all x1, waiting for transfers between devices, body(): lax.all_to_all(to_lanes(send_x), 'expert', split_axis=0, concat_axis=0, t...  21.2 us
    reduce_scatter x1, waiting for transfers between devices, body(): lax.psum_scatter(jnp.concatenate([out_part, grad_part], axis=1), 'dp', sc...  18.1 us
    all_to_all x1, starting transfers between devices, body(): lax.all_to_all(to_lanes(send_x), 'expert', split_axis=0, concat_axis=0, t...  11.8 us
    reduce_scatter x1, waiting for transfers between devices, body(): y_sum = lax.psum_scatter(y_lanes, 'dp', scatter_dimension=0, tiled=True)  7.26 us
  transfers between devices with their start and end apart: 5, of which 5 were waited for; matrix products, arithmetic and copies ran while one was open for 14% of the time, Pallas kernels for 0%

profile of v6, /device:TPU:8, one launch (start us, length us, event | category | flops | bytes accessed | tf_op | source)
XLA Modules:
  0.0 319.2 jit_solution(7358213431284104192)
XLA Ops:
  7.2 0.9 copy.32
  8.2 0.5 fusion.16
  9.2 0.4 convolution_convert_fusion.4
  9.8 1.0 copy-done.2
  10.7 0.5 broadcast.80
  11.3 2.8 reduce
  14.0 1.2 reshape.60
  15.2 11.8 %all-to-all-start = ((bf16[32,2,8960]{2,1,0:T(2,128)(2,1)}), bf16[32,2,8960]{2,1,0:T(2,128)(2,1)S(1)}, u32[]{:S(2)}, u32[]{:S(2)}) async-start(bf16[32,2,8960]{2,1,0:T(2,128)(2,1)} %reshape.60), calls=%async_computation | async-start | bytes 2293760 | tf_op jit(solution)/shard_map/all_to_all | solution.py:45
  27.4 3.0 multiply_convert_fusion
  30.4 0.7 slice_dynamic-update-slice_fusion.19
  31.1 0.7 slice_dynamic-update-slice_fusion.18
  31.8 0.7 slice_dynamic-update-slice_fusion.17
  32.5 0.7 slice_dynamic-update-slice_fusion.16
  33.3 0.7 slice_dynamic-update-slice_fusion.15
  34.0 21.2 %all-to-all-done = bf16[32,2,8960]{2,1,0:T(2,128)(2,1)S(1)} async-done(((bf16[32,2,8960]{2,1,0:T(2,128)(2,1)}), bf16[32,2,8960]{2,1,0:T(2,128)(2,1)S(1)}, u32[]{:S(2)}, u32[]{:S(2)}) %all-to-all-start) | async-done | bytes 1146912 | tf_op jit(solution)/shard_map/all_to_all | solution.py:45
  55.1 3.4 %reshape.61 = bf16[32,1,17920]{2,1,0:T(2,128)(2,1)} reshape(bf16[32,2,8960]{2,1,0:T(2,128)(2,1)S(1)} %all-to-all-done) | data formatting | bytes 2293760
  58.6 2.8 copy.48
  61.4 54.5 %all-gather.3.cloned.1.call-done = bf16[256,17920]{1,0:T(8,128)(2,1)} async-done(((bf16[32,17920]{1,0:T(8,128)(2,1)}), bf16[256,17920]{1,0:T(8,128)(2,1)}) %all-gather.3.cloned.1.call-update) | async-done | bytes 9175056 | tf_op jit(solution)/shard_map/all_gather | solution.py:48
  115.9 1.6 slice_dynamic-update-slice_fusion.14
  117.5 1.6 slice_dynamic-update-slice_fusion.13
  119.2 1.6 slice_dynamic-update-slice_fusion.12
  120.8 1.6 slice_dynamic-update-slice_fusion.11
  122.4 1.7 slice_dynamic-update-slice_fusion.10
  124.2 0.2 copy-done.10
  124.4 2.8 fusion.11
  127.2 0.8 copy-done.6
  128.0 3.9 %multiply_convert_fusion.3 = (bf16[1280,224]{0,1:T(8,128)(2,1)S(1)}, f32[1280,224]{0,1:T(8,128)}) fusion(f32[1280,224]{0,1:T(8,128)S(1)} %fusion.11, bf16[1280,3584]{1,0:T(8,128)(2,1)S(1)} %slice_dynamic-update-slice_fusion.10, bf16[1,224,3584]{2,1,0:T(8,128)(2,1)S(1)} %copy-done.11), kind=kOutput, calls=%fused_computation.43 | convolution fusion | flops 2056929280 | bytes 13647872 | tf_op jit(solution)/shard_map/dot_general | solution.py:55
  131.9 2.6 convolution_convert_fusion
  134.5 1.4 slice_dynamic-update-slice_fusion.9
  135.9 1.4 slice_dynamic-update-slice_fusion.8
  137.3 1.4 slice_dynamic-update-slice_fusion.7
  138.7 1.4 slice_dynamic-update-slice_fusion.6
  140.1 1.4 slice_dynamic-update-slice_fusion.5
  141.6 2.8 reduce.1
  144.4 1.2 reshape.62
  145.5 41.6 %all_to_all.36 = bf16[32,2,8960]{2,1,0:T(2,128)(2,1)S(1)} all-to-all(bf16[32,2,8960]{2,1,0:T(2,128)(2,1)} %reshape.62), channel_id=1, replica_groups=mesh['dp'=8,'expert'=32] {'expert'}, dimensions={0} | all-to-all | bytes 2293760 | tf_op jit(solution)/shard_map/all_to_all | solution.py:47
  187.1 3.4 %reshape.63 = bf16[32,1,17920]{2,1,0:T(2,128)(2,1)} reshape(bf16[32,2,8960]{2,1,0:T(2,128)(2,1)S(1)} %all_to_all.36) | data formatting | bytes 2293760
  190.5 2.9 copy.47
  193.4 7.3 %reduce-scatter.3.cloned.1.call-done = bf16[32,17920]{1,0:T(8,128)(2,1)} async-done(((bf16[256,17920]{1,0:T(8,128)(2,1)}), bf16[32,17920]{1,0:T(8,128)(2,1)}) %reduce-scatter.3.cloned.1.call-update) | async-done | bytes 1146896 | tf_op jit(solution)/shard_map/reduce_scatter | solution.py:63
  200.7 0.2 reduce-scatter.5.cloned.1.call-start
  200.9 2.8 reduce.2
  203.7 1.2 reshape.64
  204.9 40.9 %all_to_all.37 = bf16[32,2,8960]{2,1,0:T(2,128)(2,1)S(1)} all-to-all(bf16[32,2,8960]{2,1,0:T(2,128)(2,1)} %reshape.64), channel_id=1, replica_groups=mesh['dp'=8,'expert'=32] {'expert'}, dimensions={0} | all-to-all | bytes 2293760 | tf_op jit(solution)/shard_map/all_to_all | solution.py:66
  245.7 3.4 %reshape.65 = bf16[32,1,17920]{2,1,0:T(2,128)(2,1)} reshape(bf16[32,2,8960]{2,1,0:T(2,128)(2,1)S(1)} %all_to_all.37) | data formatting | bytes 2293760
  249.2 1.8 copy.46
  250.9 6.8 %all-gather.5.cloned.1.call-done = bf16[256,17920]{1,0:T(8,128)(2,1)} async-done(((bf16[32,17920]{1,0:T(8,128)(2,1)}), bf16[256,17920]{1,0:T(8,128)(2,1)}) %all-gather.5.cloned.1.call-update) | async-done | bytes 9175056 | tf_op jit(solution)/shard_map/all_gather | solution.py:65
  257.7 1.6 slice_dynamic-update-slice_fusion.4
  259.3 1.6 slice_dynamic-update-slice_fusion.3
  260.9 1.6 slice_dynamic-update-slice_fusion.2
  262.6 1.6 slice_dynamic-update-slice_fusion.1
  264.2 1.6 slice_dynamic-update-slice_fusion
  265.8 3.5 %copy-done.7 = bf16[1280,3584]{1,0:T(8,128)(2,1)} copy-done((bf16[1280,3584]{1,0:T(8,128)(2,1)}, bf16[1280,3584]{1,0:T(8,128)(2,1)S(1)}, u32[]{:S(2)}) %copy-start.7) | copy-done | bytes 9175064
  269.5 1.9 fusion.4
  271.4 0.3 fusion.5
  271.9 1.4 pad_maximum_fusion
  273.3 1.0 copy-done.5
  274.4 7.1 %fusion.2 = bf16[1,224,3584]{2,1,0:T(8,128)(2,1)} fusion(bf16[1280,224]{0,1:T(8,128)(2,1)S(1)} %copy-done.5, bf16[1280,3584]{1,0:T(8,128)(2,1)} %copy-done.7), kind=kOutput, calls=%fused_computation.7 | convolution fusion | flops 2056011776 | bytes 11354112 | tf_op jit(solution)/shard_map/dot_general | solution.py:76
  281.5 2.8 fusion.6
  284.4 3.5 %fusion.1 = bf16[1,224,3584]{2,1,0:T(8,128)(2,1)} fusion(bf16[1280,3584]{1,0:T(8,128)(2,1)S(1)} %bitcast.52, f32[1280,224]{0,1:T(8,128)S(1)} %fusion.6, f32[1280,224]{0,1:T(8,128)S(1)} %copy-done.13), kind=kOutput, calls=%fused_computation.6 | convolution fusion | flops 2057732096 | bytes 13074432 | tf_op jit(solution)/shard_map/dot_general | solution.py:78
  287.9 3.7 %fusion = bf16[1,224,3584]{2,1,0:T(8,128)(2,1)} fusion(bf16[1280,3584]{1,0:T(8,128)(2,1)S(1)} %bitcast.52, f32[1280,224]{0,1:T(8,128)S(1)} %copy-done.13, f32[1280,224]{0,1:T(8,128)S(1)} %fusion.6, f32[1280,224]{0,1:T(8,128)S(1)} %copy-done.14), kind=kOutput, calls=%fused_computation.5 | convolution fusion | flops 2058878976 | bytes 14221312 | tf_op jit(solution)/shard_map/dot_general | solution.py:77
  291.7 18.1 %reduce-scatter.5.cloned.1.call-done = f32[16,3592]{1,0:T(8,128)} async-done(((f32[128,3592]{1,0:T(8,128)}), f32[16,3592]{1,0:T(8,128)}) %reduce-scatter.5.cloned.1.call-update) | async-done | bytes 229904 | tf_op jit(solution)/shard_map/reduce_scatter | solution.py:88
  309.7 0.7 slice.155
  310.4 0.7 copy.39
  311.1 1.6 slice.187
  (61 shorter events, 1.4 us)
Async XLA Ops:
  7.2 124.7 %copy-start = (bf16[1,224,3584]{2,1,0:T(8,128)(2,1)S(1)}, bf16[1,224,3584]{2,1,0:T(8,128)(2,1)}, u32[]{:S(2)}) copy-start(bf16[1,224,3584]{2,1,0:T(8,128)(2,1)} %param.13) | copy-start | bytes 4816900
  7.2 2.0 copy-start.3
  9.7 1.0 copy-start.2
  15.2 11.9 %copy-start.9 = (f32[128,8]{0,1:T(8,128)S(1)}, f32[128,8]{0,1:T(8,128)}, u32[]{:S(2)}) copy-start(f32[128,8]{0,1:T(8,128)} %param.10) | copy-start | bytes 12292
  15.2 40.0 %all-to-all-start = ((bf16[32,2,8960]{2,1,0:T(2,128)(2,1)}), bf16[32,2,8960]{2,1,0:T(2,128)(2,1)S(1)}, u32[]{:S(2)}, u32[]{:S(2)}) async-start(bf16[32,2,8960]{2,1,0:T(2,128)(2,1)} %reshape.60), calls=%async_computation | async-start | bytes 2293760 | tf_op jit(solution)/shard_map/all_to_all | solution.py:45
  27.0 88.9 %all-gather.3.cloned.1.call-start = ((), (), s32[]{:S(2)}) async-start(), calls=%async_computation.5 | async-start | bytes 10321920 | tf_op jit(solution)/shard_map/all_gather | solution.py:48
  61.4 139.3 %reduce-scatter.3.cloned.1.call-start = ((), (), s32[]{:S(2)}) async-start(), calls=%async_computation.6 | async-start | bytes 10321920 | tf_op jit(solution)/shard_map/reduce_scatter | solution.py:63
  122.4 2.0 copy-start.10
  124.4 3.6 %copy-start.6 = (bf16[1280,3584]{1,0:T(8,128)(2,1)}, bf16[1280,3584]{1,0:T(8,128)(2,1)S(1)}, u32[]{:S(2)}) copy-start(bf16[1280,3584]{1,0:T(8,128)(2,1)S(1)} %slice_dynamic-update-slice_fusion.10) | copy-start | bytes 27525124
  124.4 3.6 %copy-start.11 = (bf16[1,224,3584]{2,1,0:T(8,128)(2,1)S(1)}, bf16[1,224,3584]{2,1,0:T(8,128)(2,1)}, u32[]{:S(2)}) copy-start(bf16[1,224,3584]{2,1,0:T(8,128)(2,1)} %param.12) | copy-start | bytes 4816900
  128.0 3.9 %copy-start.12 = (f32[1280,224]{0,1:T(8,128)}, f32[1280,224]{0,1:T(8,128)S(1)}, u32[]{:S(2)}) copy-start(f32[1280,224]{0,1:T(8,128)S(1)} %fusion.11) | copy-start | bytes 3440644
  131.9 2.6 copy-start.4
  141.6 116.1 %all-gather.5.cloned.1.call-start = ((), (), s32[]{:S(2)}) async-start(), calls=%async_computation.7 | async-start | bytes 10321920 | tf_op jit(solution)/shard_map/all_gather | solution.py:65
  200.7 109.0 %reduce-scatter.5.cloned.1.call-start = ((), (), s32[]{:S(2)}) async-start(), calls=%async_computation.8 | async-start | bytes 2138112 | tf_op jit(solution)/shard_map/reduce_scatter | solution.py:88
  265.8 3.5 %copy-start.7 = (bf16[1280,3584]{1,0:T(8,128)(2,1)}, bf16[1280,3584]{1,0:T(8,128)(2,1)S(1)}, u32[]{:S(2)}) copy-start(bf16[1280,3584]{1,0:T(8,128)(2,1)S(1)} %slice_dynamic-update-slice_fusion) | copy-start | bytes 27525124
  269.5 1.9 copy-start.1
  273.3 1.1 copy-start.5
  274.4 7.2 %copy-start.8 = (bf16[1280,3584]{1,0:T(8,128)(2,1)S(1)}, bf16[1280,3584]{1,0:T(8,128)(2,1)}, u32[]{:S(2)}) copy-start(bf16[1280,3584]{1,0:T(8,128)(2,1)} %copy-done.7) | copy-start | bytes 27525124
  274.4 10.0 %slice-start = ((s8[9175040]{0:T(1024)(128)(4,1)}), s8[4194304]{0:T(1024)(128)(4,1)S(1)}, s32[]{:S(2)}) async-start(s8[9175040]{0:T(1024)(128)(4,1)} %bitcast.51), calls=%async_computation.9 | async-start | bytes 8388608
  274.4 10.0 %slice-start.1 = ((s8[9175040]{0:T(1024)(128)(4,1)}), s8[4194304]{0:T(1024)(128)(4,1)S(1)}, s32[]{:S(2)}) async-start(s8[9175040]{0:T(1024)(128)(4,1)} %bitcast.51), calls=%async_computation.10 | async-start | bytes 8388608
  281.5 2.9 slice-start.2
  281.5 2.9 copy-start.13
  284.4 3.5 %copy-start.14 = (f32[1280,224]{0,1:T(8,128)S(1)}, f32[1280,224]{0,1:T(8,128)}, u32[]{:S(2)}) copy-start(f32[1280,224]{0,1:T(8,128)} %get-tuple-element.48) | copy-start | bytes 3440644
Sparse Core Ops, SparseCore 0:
  61.5 54.3 all-gather.2
  141.7 58.9 reduce-scatter.2
  202.5 55.1 all-gather.4
  273.5 36.2 reduce-scatter.4

commit v7 on v6

--- a/solution.py
+++ b/solution.py
@@ -86,10 +86,13 @@
     dot_dest = jnp.sum(cot_sel * y_home, axis=1)
     grad_part = jnp.sum(dest_hot * dot_dest[None, :], axis=1).reshape(tok_rows, top_slots)
     both_sum = lax.psum_scatter(
-        jnp.concatenate([out_part, grad_part], axis=1), "dp", scatter_dimension=0, tiled=True
+        jnp.concatenate([out_part, grad_part], axis=1).astype(jnp.bfloat16),
+        "dp",
+        scatter_dimension=0,
+        tiled=True,
     )
     layer_sum = both_sum[:, :width]
-    gate_sum = both_sum[:, width:]
+    gate_sum = both_sum[:, width:].astype(jnp.float32)
     return (
         layer_sum.astype(jnp.bfloat16),
         gate_sum,

time: 320 us -> 319 us (level)
  local copies, waits for them, and re-layouts: 59.9 us -> 54.6 us
  matrix products: 32.3 us -> 37.1 us
    unnamed x72 -> x68, local copies, waits for them, and re-layouts: 51.1 us -> 46.5 us
    dot_general x1, matrix products: 3.48 us -> 7.24 us  [body(): lax.dot_general(grad_up_pre, flat_x, by_row, preferred_element_type=jnp.f...]
where the time goes in v7:
time: 319 us; the launch traced here: 318 us
  waiting for transfers between devices  106 us (33%)
  blocking collectives  82.4 us (26%)
  local copies, waits for them, and re-layouts  54.6 us (17%)
  matrix products  37.1 us (12%)
  between operations  14.1 us (4%)
  starting transfers between devices  12.2 us (4%)
  other arithmetic  10.8 us (3%)
    all_gather x1, waiting for transfers between devices, body(): flat_x = lanes_to_rows(lax.all_gather(recv_x, 'dp', axis=0, tiled=True))  54.5 us
    unnamed x68, local copies, waits for them, and re-layouts  46.5 us
    all_to_all x1, blocking collectives, body(): lax.all_to_all(lanes_dy, 'expert', split_axis=0, concat_axis=0, tiled=True)  41.6 us
    all_to_all x1, blocking collectives, body(): lax.all_to_all(y_sum, 'expert', split_axis=0, concat_axis=0, tiled=True)  40.9 us
    all_to_all x1, waiting for transfers between devices, body(): lax.all_to_all(to_lanes(send_x), 'expert', split_axis=0, concat_axis=0, t...  21.1 us
    reduce_scatter x1, waiting for transfers between devices, body(): lax.psum_scatter(jnp.concatenate([out_part, grad_part], axis=1).astype(jn...  16.8 us
    all_to_all x1, starting transfers between devices, body(): lax.all_to_all(to_lanes(send_x), 'expert', split_axis=0, concat_axis=0, t...  11.8 us
    reduce_scatter x1, waiting for transfers between devices, body(): y_sum = lax.psum_scatter(y_lanes, 'dp', scatter_dimension=0, tiled=True)  7.27 us
  transfers between devices with their start and end apart: 5, of which 5 were waited for; matrix products, arithmetic and copies ran while one was open for 14% of the time, Pallas kernels for 0%

profile of v7, /device:TPU:8, one launch (start us, length us, event | category | flops | bytes accessed | tf_op | source)
XLA Modules:
  0.0 317.7 jit_solution(16067175609506990739)
XLA Ops:
  7.2 0.9 copy.32
  8.2 0.5 fusion.15
  9.2 0.4 convolution_convert_fusion.4
  9.8 1.0 copy-done.2
  10.7 0.5 broadcast.80
  11.3 2.8 reduce
  14.0 1.2 reshape.61
  15.2 11.8 %all-to-all-start = ((bf16[32,2,8960]{2,1,0:T(2,128)(2,1)}), bf16[32,2,8960]{2,1,0:T(2,128)(2,1)S(1)}, u32[]{:S(2)}, u32[]{:S(2)}) async-start(bf16[32,2,8960]{2,1,0:T(2,128)(2,1)} %reshape.61), calls=%async_computation | async-start | bytes 2293760 | tf_op jit(solution)/shard_map/all_to_all | solution.py:45
  27.3 0.2 select_reduce_fusion.1
  27.4 3.0 multiply_convert_fusion
  30.4 0.7 slice_dynamic-update-slice_fusion.19
  31.1 0.7 slice_dynamic-update-slice_fusion.18
  31.9 0.7 slice_dynamic-update-slice_fusion.17
  32.6 0.7 slice_dynamic-update-slice_fusion.16
  33.3 0.7 slice_dynamic-update-slice_fusion.15
  34.0 21.1 %all-to-all-done = bf16[32,2,8960]{2,1,0:T(2,128)(2,1)S(1)} async-done(((bf16[32,2,8960]{2,1,0:T(2,128)(2,1)}), bf16[32,2,8960]{2,1,0:T(2,128)(2,1)S(1)}, u32[]{:S(2)}, u32[]{:S(2)}) %all-to-all-start) | async-done | bytes 1146912 | tf_op jit(solution)/shard_map/all_to_all | solution.py:45
  55.1 3.4 %reshape.62 = bf16[32,1,17920]{2,1,0:T(2,128)(2,1)} reshape(bf16[32,2,8960]{2,1,0:T(2,128)(2,1)S(1)} %all-to-all-done) | data formatting | bytes 2293760
  58.6 2.8 copy.48
  61.4 54.5 %all-gather.3.cloned.1.call-done = bf16[256,17920]{1,0:T(8,128)(2,1)} async-done(((bf16[32,17920]{1,0:T(8,128)(2,1)}), bf16[256,17920]{1,0:T(8,128)(2,1)}) %all-gather.3.cloned.1.call-update) | async-done | bytes 9175056 | tf_op jit(solution)/shard_map/all_gather | solution.py:48
  115.9 1.6 slice_dynamic-update-slice_fusion.14
  117.5 1.6 slice_dynamic-update-slice_fusion.13
  119.1 1.6 slice_dynamic-update-slice_fusion.12
  120.8 1.6 slice_dynamic-update-slice_fusion.11
  122.4 1.7 slice_dynamic-update-slice_fusion.10
  124.1 0.2 copy-done.7
  124.4 2.8 fusion.10
  127.2 0.8 copy-done.4
  128.0 3.9 %multiply_convert_fusion.3 = (bf16[1280,224]{0,1:T(8,128)(2,1)S(1)}, f32[1280,224]{0,1:T(8,128)}) fusion(f32[1280,224]{0,1:T(8,128)S(1)} %fusion.10, bf16[1280,3584]{1,0:T(8,128)(2,1)S(1)} %slice_dynamic-update-slice_fusion.10, bf16[1,224,3584]{2,1,0:T(8,128)(2,1)S(1)} %copy-done.8), kind=kOutput, calls=%fused_computation.42 | convolution fusion | flops 2056929280 | bytes 13647872 | tf_op jit(solution)/shard_map/dot_general | solution.py:55
  131.8 2.6 convolution_convert_fusion
  134.4 1.4 slice_dynamic-update-slice_fusion.9
  135.9 1.4 slice_dynamic-update-slice_fusion.8
  137.3 1.4 slice_dynamic-update-slice_fusion.7
  138.6 1.4 slice_dynamic-update-slice_fusion.6
  140.1 1.4 slice_dynamic-update-slice_fusion.5
  141.5 2.8 reduce.1
  144.3 1.2 reshape.63
  145.5 41.6 %all_to_all.36 = bf16[32,2,8960]{2,1,0:T(2,128)(2,1)S(1)} all-to-all(bf16[32,2,8960]{2,1,0:T(2,128)(2,1)} %reshape.63), channel_id=1, replica_groups=mesh['dp'=8,'expert'=32] {'expert'}, dimensions={0} | all-to-all | bytes 2293760 | tf_op jit(solution)/shard_map/all_to_all | solution.py:47
  187.0 3.4 %reshape.64 = bf16[32,1,17920]{2,1,0:T(2,128)(2,1)} reshape(bf16[32,2,8960]{2,1,0:T(2,128)(2,1)S(1)} %all_to_all.36) | data formatting | bytes 2293760
  190.5 2.9 copy.47
  193.4 7.3 %reduce-scatter.3.cloned.1.call-done = bf16[32,17920]{1,0:T(8,128)(2,1)} async-done(((bf16[256,17920]{1,0:T(8,128)(2,1)}), bf16[32,17920]{1,0:T(8,128)(2,1)}) %reduce-scatter.3.cloned.1.call-update) | async-done | bytes 1146896 | tf_op jit(solution)/shard_map/reduce_scatter | solution.py:63
  200.7 0.2 reduce-scatter.5.cloned.1.call-start
  200.9 2.8 reduce.2
  203.7 1.2 reshape.65
  204.8 40.9 %all_to_all.37 = bf16[32,2,8960]{2,1,0:T(2,128)(2,1)S(1)} all-to-all(bf16[32,2,8960]{2,1,0:T(2,128)(2,1)} %reshape.65), channel_id=1, replica_groups=mesh['dp'=8,'expert'=32] {'expert'}, dimensions={0} | all-to-all | bytes 2293760 | tf_op jit(solution)/shard_map/all_to_all | solution.py:66
  245.7 3.4 %reshape.66 = bf16[32,1,17920]{2,1,0:T(2,128)(2,1)} reshape(bf16[32,2,8960]{2,1,0:T(2,128)(2,1)S(1)} %all_to_all.37) | data formatting | bytes 2293760
  249.1 1.8 copy.46
  250.9 6.8 %all-gather.5.cloned.1.call-done = bf16[256,17920]{1,0:T(8,128)(2,1)} async-done(((bf16[32,17920]{1,0:T(8,128)(2,1)}), bf16[256,17920]{1,0:T(8,128)(2,1)}) %all-gather.5.cloned.1.call-update) | async-done | bytes 9175056 | tf_op jit(solution)/shard_map/all_gather | solution.py:65
  257.7 1.6 slice_dynamic-update-slice_fusion.4
  259.3 1.6 slice_dynamic-update-slice_fusion.3
  260.9 1.6 slice_dynamic-update-slice_fusion.2
  262.5 1.6 slice_dynamic-update-slice_fusion.1
  264.1 1.6 slice_dynamic-update-slice_fusion
  265.8 3.9 %fusion.5 = f32[1280,224]{0,1:T(8,128)} fusion(bf16[1280,3584]{1,0:T(8,128)(2,1)S(1)} %slice_dynamic-update-slice_fusion, bf16[1,224,3584]{2,1,0:T(8,128)(2,1)S(1)} %copy-done), kind=kOutput, calls=%fused_computation.30 | convolution fusion | flops 2055208960 | bytes 11927552 | tf_op jit(solution)/shard_map/dot_general | solution.py:69
  269.8 1.9 convolution_convert_fusion.5
  271.7 0.3 fusion.4
  272.0 0.2 select_reduce_fusion
  272.3 1.0 pad_maximum_fusion
  273.3 7.2 %fusion.2 = bf16[1,224,3584]{2,1,0:T(8,128)(2,1)} fusion(bf16[1280,224]{0,1:T(8,128)(2,1)S(1)} %get-tuple-element.47, bf16[1280,3584]{1,0:T(8,128)(2,1)} %copy-done.5), kind=kOutput, calls=%fused_computation.7 | convolution fusion | flops 2056011776 | bytes 11354112 | tf_op jit(solution)/shard_map/dot_general | solution.py:76
  280.5 7.2 %fusion.1 = bf16[1,224,3584]{2,1,0:T(8,128)(2,1)} fusion(bf16[1280,3584]{1,0:T(8,128)(2,1)} %copy-done.4, f32[1280,224]{0,1:T(8,128)S(1)} %copy-done.11, f32[1280,224]{0,1:T(8,128)S(1)} %copy-done.10), kind=kOutput, calls=%fused_computation.6 | convolution fusion | flops 2057732096 | bytes 13074432 | tf_op jit(solution)/shard_map/dot_general | solution.py:78
  287.8 3.7 %fusion = bf16[1,224,3584]{2,1,0:T(8,128)(2,1)} fusion(bf16[1280,3584]{1,0:T(8,128)(2,1)S(1)} %bitcast.52, f32[1280,224]{0,1:T(8,128)S(1)} %copy-done.10, f32[1280,224]{0,1:T(8,128)S(1)} %copy-done.11, f32[1280,224]{0,1:T(8,128)S(1)} %copy-done.12), kind=kOutput, calls=%fused_computation.5 | convolution fusion | flops 2058878976 | bytes 14221312 | tf_op jit(solution)/shard_map/dot_general | solution.py:77
  291.5 16.8 %reduce-scatter.5.cloned.1.call-done = bf16[16,3592]{1,0:T(8,128)(2,1)} async-done(((bf16[128,3592]{1,0:T(8,128)(2,1)}), bf16[16,3592]{1,0:T(8,128)(2,1)}) %reduce-scatter.5.cloned.1.call-update) | async-done | bytes 114960 | tf_op jit(solution)/shard_map/reduce_scatter | solution.py:88
  308.2 0.7 slice_convert_fusion
  308.9 0.7 copy.39
  309.6 1.6 slice.153
  (57 shorter events, 1.1 us)
Async XLA Ops:
  7.2 124.7 %copy-start = (bf16[1,224,3584]{2,1,0:T(8,128)(2,1)S(1)}, bf16[1,224,3584]{2,1,0:T(8,128)(2,1)}, u32[]{:S(2)}) copy-start(bf16[1,224,3584]{2,1,0:T(8,128)(2,1)} %param.13) | copy-start | bytes 4816900
  7.2 2.0 copy-start.3
  9.7 1.0 copy-start.2
  15.2 11.9 %copy-start.6 = (f32[128,8]{0,1:T(8,128)S(1)}, f32[128,8]{0,1:T(8,128)}, u32[]{:S(2)}) copy-start(f32[128,8]{0,1:T(8,128)} %param.10) | copy-start | bytes 12292
  15.2 40.0 %all-to-all-start = ((bf16[32,2,8960]{2,1,0:T(2,128)(2,1)}), bf16[32,2,8960]{2,1,0:T(2,128)(2,1)S(1)}, u32[]{:S(2)}, u32[]{:S(2)}) async-start(bf16[32,2,8960]{2,1,0:T(2,128)(2,1)} %reshape.61), calls=%async_computation | async-start | bytes 2293760 | tf_op jit(solution)/shard_map/all_to_all | solution.py:45
  27.0 88.9 %all-gather.3.cloned.1.call-start = ((), (), s32[]{:S(2)}) async-start(), calls=%async_computation.5 | async-start | bytes 10321920 | tf_op jit(solution)/shard_map/all_gather | solution.py:48
  61.4 139.3 %reduce-scatter.3.cloned.1.call-start = ((), (), s32[]{:S(2)}) async-start(), calls=%async_computation.6 | async-start | bytes 10321920 | tf_op jit(solution)/shard_map/reduce_scatter | solution.py:63
  122.4 2.0 copy-start.7
  124.4 3.6 %copy-start.4 = (bf16[1280,3584]{1,0:T(8,128)(2,1)}, bf16[1280,3584]{1,0:T(8,128)(2,1)S(1)}, u32[]{:S(2)}) copy-start(bf16[1280,3584]{1,0:T(8,128)(2,1)S(1)} %slice_dynamic-update-slice_fusion.10) | copy-start | bytes 27525124
  124.4 3.6 %copy-start.8 = (bf16[1,224,3584]{2,1,0:T(8,128)(2,1)S(1)}, bf16[1,224,3584]{2,1,0:T(8,128)(2,1)}, u32[]{:S(2)}) copy-start(bf16[1,224,3584]{2,1,0:T(8,128)(2,1)} %param.12) | copy-start | bytes 4816900
  128.0 3.9 %copy-start.9 = (f32[1280,224]{0,1:T(8,128)}, f32[1280,224]{0,1:T(8,128)S(1)}, u32[]{:S(2)}) copy-start(f32[1280,224]{0,1:T(8,128)S(1)} %fusion.10) | copy-start | bytes 3440644
  141.5 116.2 %all-gather.5.cloned.1.call-start = ((), (), s32[]{:S(2)}) async-start(), calls=%async_computation.7 | async-start | bytes 10321920 | tf_op jit(solution)/shard_map/all_gather | solution.py:65
  200.7 107.6 %reduce-scatter.5.cloned.1.call-start = ((), (), s32[]{:S(2)}) async-start(), calls=%async_computation.8 | async-start | bytes 1069056 | tf_op jit(solution)/shard_map/reduce_scatter | solution.py:88
  265.8 3.9 %copy-start.5 = (bf16[1280,3584]{1,0:T(8,128)(2,1)}, bf16[1280,3584]{1,0:T(8,128)(2,1)S(1)}, u32[]{:S(2)}) copy-start(bf16[1280,3584]{1,0:T(8,128)(2,1)S(1)} %slice_dynamic-update-slice_fusion) | copy-start | bytes 27525124
  269.7 1.9 copy-start.1
  273.3 7.2 %copy-start.10 = (f32[1280,224]{0,1:T(8,128)S(1)}, f32[1280,224]{0,1:T(8,128)}, u32[]{:S(2)}) copy-start(f32[1280,224]{0,1:T(8,128)} %copy-done.9) | copy-start | bytes 3440644
  273.3 7.2 %copy-start.11 = (f32[1280,224]{0,1:T(8,128)S(1)}, f32[1280,224]{0,1:T(8,128)}, u32[]{:S(2)}) copy-start(f32[1280,224]{0,1:T(8,128)} %fusion.5) | copy-start | bytes 3440644
  273.3 14.4 %slice-start = ((s8[9175040]{0:T(1024)(128)(4,1)}), s8[4194304]{0:T(1024)(128)(4,1)S(1)}, s32[]{:S(2)}) async-start(s8[9175040]{0:T(1024)(128)(4,1)} %bitcast.51), calls=%async_computation.9 | async-start | bytes 8388608
  273.3 14.4 %slice-start.1 = ((s8[9175040]{0:T(1024)(128)(4,1)}), s8[4194304]{0:T(1024)(128)(4,1)S(1)}, s32[]{:S(2)}) async-start(s8[9175040]{0:T(1024)(128)(4,1)} %bitcast.51), calls=%async_computation.10 | async-start | bytes 8388608
  280.5 7.3 %slice-start.2 = ((s8[9175040]{0:T(1024)(128)(4,1)}), s8[786432]{0:T(1024)(128)(4,1)S(1)}, s32[]{:S(2)}) async-start(s8[9175040]{0:T(1024)(128)(4,1)} %bitcast.51), calls=%async_computation.11 | async-start | bytes 1572864
  280.5 7.3 %copy-start.12 = (f32[1280,224]{0,1:T(8,128)S(1)}, f32[1280,224]{0,1:T(8,128)}, u32[]{:S(2)}) copy-start(f32[1280,224]{0,1:T(8,128)} %get-tuple-element.48) | copy-start | bytes 3440644
Sparse Core Ops, SparseCore 0:
  61.5 54.3 all-gather.2
  141.6 58.9 reduce-scatter.2
  202.5 55.1 all-gather.4
  273.4 34.7 reduce-scatter.4

commit v8 on v7

--- a/solution.py
+++ b/solution.py
@@ -45,21 +45,42 @@
     recv_x = lax.all_to_all(to_lanes(send_x), "expert", split_axis=0, concat_axis=0, tiled=True)
     recv_x, lanes_dy = lax.optimization_barrier((recv_x, to_lanes(send_dy)))
     recv_dy = lax.all_to_all(lanes_dy, "expert", split_axis=0, concat_axis=0, tiled=True)
-    flat_x = lanes_to_rows(lax.all_gather(recv_x, "dp", axis=0, tiled=True))
+    gathered_x = lax.all_gather(recv_x, "dp", axis=0, tiled=True)
+    x_chunks = [gathered_x[:, r * width : (r + 1) * width] for r in range(share)]
     gate_local = w_gate[0]
     up_local = w_up[0]
     down_local = w_down[0]
     by_feature = (((1,), (1,)), ((), ()))
     by_row = (((0,), (0,)), ((), ()))
-    gate_pre = lax.dot_general(flat_x, gate_local, by_feature, preferred_element_type=jnp.float32)
-    up_pre = lax.dot_general(flat_x, up_local, by_feature, preferred_element_type=jnp.float32)
+    gate_pre = jnp.concatenate(
+        [
+            lax.dot_general(xc, gate_local, by_feature, preferred_element_type=jnp.float32)
+            for xc in x_chunks
+        ],
+        axis=0,
+    )
+    up_pre = jnp.concatenate(
+        [
+            lax.dot_general(xc, up_local, by_feature, preferred_element_type=jnp.float32)
+            for xc in x_chunks
+        ],
+        axis=0,
+    )
     sigma_gate = jax.nn.sigmoid(gate_pre)
     hidden = (gate_pre * sigma_gate * up_pre).astype(jnp.bfloat16)
-    y_part = jnp.dot(hidden, down_local, preferred_element_type=jnp.float32).astype(jnp.bfloat16)
     stack_rows = dp_count * groups
     y_lanes = jnp.concatenate(
-        [y_part[r * stack_rows : (r + 1) * stack_rows] for r in range(share)], axis=1
+        [
+            jnp.dot(
+                hidden[r * stack_rows : (r + 1) * stack_rows],
+                down_local,
+                preferred_element_type=jnp.float32,
+            ).astype(jnp.bfloat16)
+            for r in range(share)
+        ],
+        axis=1,
     )
+    flat_x = jnp.concatenate(x_chunks, axis=0)
     y_sum = lax.psum_scatter(y_lanes, "dp", scatter_dimension=0, tiled=True)
     y_sum, recv_dy = lax.optimization_barrier((y_sum, recv_dy))
     flat_dy = lanes_to_rows(lax.all_gather(recv_dy, "dp", axis=0, tiled=True))

time: 319 us -> 317 us (level)
  blocking collectives: 82.4 us -> 41.6 us
  waiting for transfers between devices: 106 us -> 126 us
  starting transfers between devices: 12.2 us -> 22.1 us
  matrix products: 37.1 us -> 46.1 us
    all_to_all x1 -> x0, blocking collectives: 40.9 us -> none  [body(): lax.all_to_all(y_sum, 'expert', split_axis=0, concat_axis=0, tiled=True)]
    all_to_all x0 -> x1, waiting for transfers between devices: none -> 18.9 us  [body(): lax.all_to_all(y_sum, 'expert', split_axis=0, concat_axis=0, tiled=True)]
    dot_general x3 -> x15, matrix products: 9.29 us -> 21.9 us  [the longest x5 9.62 us: body(): jnp.dot(hidden[r * stack_rows:(r + 1) * stack_rows], down_local, preferre...]
    all_to_all x0 -> x1, starting transfers between devices: none -> 10.1 us  [body(): lax.all_to_all(y_sum, 'expert', split_axis=0, concat_axis=0, tiled=True)]
    dot_general x1, matrix products: 7.24 us -> 3.48 us  [body(): lax.dot_general(grad_up_pre, flat_x, by_row, preferred_element_type=jnp.f...]
    reduce_scatter x1, waiting for transfers between devices: 16.8 us -> 20.5 us  [body(): lax.psum_scatter(jnp.concatenate([out_part, grad_part], axis=1).astype(jn...]
  transfers between devices with their start and end apart: 5 -> 6, of which waited for: 5 -> 6; matrix products, arithmetic and copies ran while one was open for 14% -> 17% of each run, Pallas kernels for 0% -> 0%
where the time goes in v8:
time: 317 us; the launch traced here: 316 us
  waiting for transfers between devices  126 us (40%)
  local copies, waits for them, and re-layouts  54.7 us (17%)
  matrix products  46.1 us (15%)
  blocking collectives  41.6 us (13%)
  starting transfers between devices  22.1 us (7%)
  between operations  14.3 us (5%)
  other arithmetic  11.1 us (4%)
    all_gather x1, waiting for transfers between devices, body(): gathered_x = lax.all_gather(recv_x, 'dp', axis=0, tiled=True)  54.5 us
    unnamed x68, local copies, waits for them, and re-layouts  46.8 us
    all_to_all x1, blocking collectives, body(): lax.all_to_all(lanes_dy, 'expert', split_axis=0, concat_axis=0, tiled=True)  41.6 us
    all_to_all x1, waiting for transfers between devices, body(): lax.all_to_all(to_lanes(send_x), 'expert', split_axis=0, concat_axis=0, t...  21.2 us
    reduce_scatter x1, waiting for transfers between devices, body(): lax.psum_scatter(jnp.concatenate([out_part, grad_part], axis=1).astype(jn...  20.5 us
    all_to_all x1, waiting for transfers between devices, body(): lax.all_to_all(y_sum, 'expert', split_axis=0, concat_axis=0, tiled=True)  18.9 us
    all_to_all x1, starting transfers between devices, body(): lax.all_to_all(to_lanes(send_x), 'expert', split_axis=0, concat_axis=0, t...  11.8 us
    all_to_all x1, starting transfers between devices, body(): lax.all_to_all(y_sum, 'expert', split_axis=0, concat_axis=0, tiled=True)  10.1 us
  transfers between devices with their start and end apart: 6, of which 6 were waited for; matrix products, arithmetic and copies ran while one was open for 17% of the time, Pallas kernels for 0%

profile of v8, /device:TPU:8, one launch (start us, length us, event | category | flops | bytes accessed | tf_op | source)
XLA Modules:
  0.0 315.9 jit_solution(5336384310232286521)
XLA Ops:
  7.2 0.9 copy.32
  9.8 1.0 copy-done.3
  11.3 2.8 reduce
  14.0 1.2 reshape.61
  15.2 11.8 %all-to-all-start = ((bf16[32,2,8960]{2,1,0:T(2,128)(2,1)}), bf16[32,2,8960]{2,1,0:T(2,128)(2,1)S(1)}, u32[]{:S(2)}, u32[]{:S(2)}) async-start(bf16[32,2,8960]{2,1,0:T(2,128)(2,1)} %reshape.61), calls=%async_computation | async-start | bytes 2293760 | tf_op jit(solution)/shard_map/all_to_all | solution.py:45
  27.4 3.0 multiply_convert_fusion
  30.5 0.7 slice_dynamic-update-slice_fusion.14
  31.2 0.7 slice_dynamic-update-slice_fusion.13
  31.9 0.7 slice_dynamic-update-slice_fusion.12
  32.6 0.7 slice_dynamic-update-slice_fusion.11
  33.3 0.7 slice_dynamic-update-slice_fusion.10
  34.0 21.2 %all-to-all-done = bf16[32,2,8960]{2,1,0:T(2,128)(2,1)S(1)} async-done(((bf16[32,2,8960]{2,1,0:T(2,128)(2,1)}), bf16[32,2,8960]{2,1,0:T(2,128)(2,1)S(1)}, u32[]{:S(2)}, u32[]{:S(2)}) %all-to-all-start) | async-done | bytes 1146912 | tf_op jit(solution)/shard_map/all_to_all | solution.py:45
  55.1 3.4 %reshape.62 = bf16[32,1,17920]{2,1,0:T(2,128)(2,1)} reshape(bf16[32,2,8960]{2,1,0:T(2,128)(2,1)S(1)} %all-to-all-done) | data formatting | bytes 2293760
  58.6 2.9 copy.48
  61.5 54.5 %all-gather.3.cloned.1.call-done = bf16[256,17920]{1,0:T(8,128)(2,1)} async-done(((bf16[32,17920]{1,0:T(8,128)(2,1)}), bf16[256,17920]{1,0:T(8,128)(2,1)}) %all-gather.3.cloned.1.call-update) | async-done | bytes 9175056 | tf_op jit(solution)/shard_map/all_gather | solution.py:48
  116.0 2.4 fusion.72
  118.4 2.7 fusion.77
  121.1 2.2 fusion.82
  123.3 0.7 fusion.87
  124.0 0.7 fusion.92
  124.8 0.7 copy-done.13
  125.5 0.7 fusion.47
  126.2 0.7 fusion.52
  126.9 0.7 fusion.57
  127.6 0.7 fusion.62
  128.3 0.7 fusion.67
  129.4 1.9 fusion.4
  131.3 1.9 fusion.3
  133.2 1.9 fusion.2
  135.1 1.9 fusion.1
  137.1 2.0 fusion
  139.1 2.8 reduce.1
  141.9 1.2 reshape.63
  143.0 41.6 %all_to_all.36 = bf16[32,2,8960]{2,1,0:T(2,128)(2,1)S(1)} all-to-all(bf16[32,2,8960]{2,1,0:T(2,128)(2,1)} %reshape.63), channel_id=1, replica_groups=mesh['dp'=8,'expert'=32] {'expert'}, dimensions={0} | all-to-all | bytes 2293760 | tf_op jit(solution)/shard_map/all_to_all | solution.py:47
  184.6 3.4 %reshape.64 = bf16[32,1,17920]{2,1,0:T(2,128)(2,1)} reshape(bf16[32,2,8960]{2,1,0:T(2,128)(2,1)S(1)} %all_to_all.36) | data formatting | bytes 2293760
  188.0 2.9 copy.47
  190.9 7.3 %reduce-scatter.3.cloned.1.call-done = bf16[32,17920]{1,0:T(8,128)(2,1)} async-done(((bf16[256,17920]{1,0:T(8,128)(2,1)}), bf16[32,17920]{1,0:T(8,128)(2,1)}) %reduce-scatter.3.cloned.1.call-update) | async-done | bytes 1146896 | tf_op jit(solution)/shard_map/reduce_scatter | solution.py:84
  198.2 1.6 slice_dynamic-update-slice_fusion.9
  199.8 1.6 slice_dynamic-update-slice_fusion.8
  201.5 3.6 %copy-done.9 = bf16[1280,3584]{1,0:T(8,128)(2,1)} copy-done((bf16[1280,3584]{1,0:T(8,128)(2,1)}, bf16[1280,3584]{1,0:T(8,128)(2,1)S(1)}, u32[]{:S(2)}) %copy-start.9) | copy-done | bytes 9175064
  205.1 2.8 reduce.2
  207.9 1.2 reshape.65
  209.0 10.1 %all-to-all-start.2 = ((bf16[32,2,8960]{2,1,0:T(2,128)(2,1)}), bf16[32,2,8960]{2,1,0:T(2,128)(2,1)S(1)}, u32[]{:S(2)}, u32[]{:S(2)}) async-start(bf16[32,2,8960]{2,1,0:T(2,128)(2,1)} %reshape.65), calls=%async_computation.3 | async-start | bytes 2293760 | tf_op jit(solution)/shard_map/all_to_all | solution.py:87
  219.2 2.9 slice_dynamic-update-slice_fusion.7
  222.1 3.0 slice_dynamic-update-slice_fusion.6
  225.1 2.9 slice_dynamic-update-slice_fusion.5
  228.0 18.9 %all-to-all-done.2 = bf16[32,2,8960]{2,1,0:T(2,128)(2,1)S(1)} async-done(((bf16[32,2,8960]{2,1,0:T(2,128)(2,1)}), bf16[32,2,8960]{2,1,0:T(2,128)(2,1)S(1)}, u32[]{:S(2)}, u32[]{:S(2)}) %all-to-all-start.2) | async-done | bytes 1146912 | tf_op jit(solution)/shard_map/all_to_all | solution.py:87
  247.0 3.4 %reshape.66 = bf16[32,1,17920]{2,1,0:T(2,128)(2,1)} reshape(bf16[32,2,8960]{2,1,0:T(2,128)(2,1)S(1)} %all-to-all-done.2) | data formatting | bytes 2293760
  250.4 1.8 copy.46
  252.1 3.6 %all-gather.5.cloned.1.call-done = bf16[256,17920]{1,0:T(8,128)(2,1)} async-done(((bf16[32,17920]{1,0:T(8,128)(2,1)}), bf16[256,17920]{1,0:T(8,128)(2,1)}) %all-gather.5.cloned.1.call-update) | async-done | bytes 9175056 | tf_op jit(solution)/shard_map/all_gather | solution.py:86
  255.8 1.6 slice_dynamic-update-slice_fusion.4
  257.4 1.6 slice_dynamic-update-slice_fusion.3
  259.0 1.6 slice_dynamic-update-slice_fusion.2
  260.6 1.6 slice_dynamic-update-slice_fusion.1
  262.3 1.6 slice_dynamic-update-slice_fusion
  263.9 4.0 %fusion.10 = f32[1280,224]{0,1:T(8,128)} fusion(bf16[1280,3584]{1,0:T(8,128)(2,1)S(1)} %slice_dynamic-update-slice_fusion, bf16[1,224,3584]{2,1,0:T(8,128)(2,1)S(1)} %copy-done), kind=kOutput, calls=%fused_computation.29 | convolution fusion | flops 2055208960 | bytes 11927552 | tf_op jit(solution)/shard_map/dot_general | solution.py:90
  268.0 1.9 convolution_convert_fusion.9
  270.5 1.0 pad_maximum_fusion
  271.6 7.2 %fusion.7 = bf16[1,224,3584]{2,1,0:T(8,128)(2,1)} fusion(bf16[1280,224]{0,1:T(8,128)(2,1)S(1)} %multiply_convert_fusion.3, bf16[1280,3584]{1,0:T(8,128)(2,1)} %copy-done.10), kind=kOutput, calls=%fused_computation.16 | convolution fusion | flops 2056011776 | bytes 11354112 | tf_op jit(solution)/shard_map/dot_general | solution.py:97
  278.8 3.5 %fusion.6 = bf16[1,224,3584]{2,1,0:T(8,128)(2,1)} fusion(bf16[1280,3584]{1,0:T(8,128)(2,1)S(1)} %bitcast.91, f32[1280,224]{0,1:T(8,128)S(1)} %copy-done.14, f32[1280,224]{0,1:T(8,128)S(1)} %copy-done.7), kind=kOutput, calls=%fused_computation.15 | convolution fusion | flops 2057732096 | bytes 13074432 | tf_op jit(solution)/shard_map/dot_general | solution.py:99
  282.3 3.7 %fusion.5 = bf16[1,224,3584]{2,1,0:T(8,128)(2,1)} fusion(bf16[1280,3584]{1,0:T(8,128)(2,1)S(1)} %bitcast.91, f32[1280,224]{0,1:T(8,128)S(1)} %copy-done.7, f32[1280,224]{0,1:T(8,128)S(1)} %copy-done.14, f32[1280,224]{0,1:T(8,128)S(1)} %copy-done.5), kind=kOutput, calls=%fused_computation.14 | convolution fusion | flops 2058878976 | bytes 14221312 | tf_op jit(solution)/shard_map/dot_general | solution.py:98
  286.0 20.5 %reduce-scatter.5.cloned.1.call-done = bf16[16,3592]{1,0:T(8,128)(2,1)} async-done(((bf16[128,3592]{1,0:T(8,128)(2,1)}), bf16[16,3592]{1,0:T(8,128)(2,1)}) %reduce-scatter.5.cloned.1.call-update) | async-done | bytes 114960 | tf_op jit(solution)/shard_map/reduce_scatter | solution.py:109
  306.5 0.7 slice_convert_fusion
  307.8 1.6 slice.153
  (70 shorter events, 4.3 us)
Async XLA Ops:
  7.2 122.2 %copy-start = (bf16[1,224,3584]{2,1,0:T(8,128)(2,1)S(1)}, bf16[1,224,3584]{2,1,0:T(8,128)(2,1)}, u32[]{:S(2)}) copy-start(bf16[1,224,3584]{2,1,0:T(8,128)(2,1)} %param.13) | copy-start | bytes 4816900
  7.2 2.0 copy-start.8
  9.7 1.0 copy-start.3
  15.2 11.9 %copy-start.11 = (f32[128,8]{0,1:T(8,128)S(1)}, f32[128,8]{0,1:T(8,128)}, u32[]{:S(2)}) copy-start(f32[128,8]{0,1:T(8,128)} %param.10) | copy-start | bytes 12292
  15.2 40.0 %all-to-all-start = ((bf16[32,2,8960]{2,1,0:T(2,128)(2,1)}), bf16[32,2,8960]{2,1,0:T(2,128)(2,1)S(1)}, u32[]{:S(2)}, u32[]{:S(2)}) async-start(bf16[32,2,8960]{2,1,0:T(2,128)(2,1)} %reshape.61), calls=%async_computation | async-start | bytes 2293760 | tf_op jit(solution)/shard_map/all_to_all | solution.py:45
  27.0 89.0 %all-gather.3.cloned.1.call-start = ((), (), s32[]{:S(2)}) async-start(), calls=%async_computation.5 | async-start | bytes 10321920 | tf_op jit(solution)/shard_map/all_gather | solution.py:48
  58.6 57.4 %copy-start.12 = (bf16[1,224,3584]{2,1,0:T(8,128)(2,1)S(1)}, bf16[1,224,3584]{2,1,0:T(8,128)(2,1)}, u32[]{:S(2)}) copy-start(bf16[1,224,3584]{2,1,0:T(8,128)(2,1)} %param.12) | copy-start | bytes 4816900
  61.5 136.7 %reduce-scatter.3.cloned.1.call-start = ((), (), s32[]{:S(2)}) async-start(), calls=%async_computation.6 | async-start | bytes 10321920 | tf_op jit(solution)/shard_map/reduce_scatter | solution.py:84
  116.0 7.3 %copy-start.1 = (bf16[256,17920]{1,0:T(8,128)(2,1)S(1)}, bf16[256,17920]{1,0:T(8,128)(2,1)}, u32[]{:S(2)}) copy-start(bf16[256,17920]{1,0:T(8,128)(2,1)} %all-gather.3.cloned.1.call-done) | copy-start | bytes 27525124
  124.0 1.4 copy-start.13
  125.5 3.6 %copy-start.4 = (f32[1280,224]{0,1:T(8,128)}, f32[1280,224]{0,1:T(8,128)S(1)}, u32[]{:S(2)}) copy-start(f32[1280,224]{0,1:T(8,128)S(1)} %fusion.92) | copy-start | bytes 3440644
  129.0 2.3 copy-start.6
  139.0 116.7 %all-gather.5.cloned.1.call-start = ((), (), s32[]{:S(2)}) async-start(), calls=%async_computation.7 | async-start | bytes 10321920 | tf_op jit(solution)/shard_map/all_gather | solution.py:86
  201.5 3.6 %copy-start.9 = (bf16[1280,3584]{1,0:T(8,128)(2,1)}, bf16[1280,3584]{1,0:T(8,128)(2,1)S(1)}, u32[]{:S(2)}) copy-start(bf16[1280,3584]{1,0:T(8,128)(2,1)S(1)} %slice_dynamic-update-slice_fusion.8) | copy-start | bytes 27525124
  209.0 37.9 %all-to-all-start.2 = ((bf16[32,2,8960]{2,1,0:T(2,128)(2,1)}), bf16[32,2,8960]{2,1,0:T(2,128)(2,1)S(1)}, u32[]{:S(2)}, u32[]{:S(2)}) async-start(bf16[32,2,8960]{2,1,0:T(2,128)(2,1)} %reshape.65), calls=%async_computation.3 | async-start | bytes 2293760 | tf_op jit(solution)/shard_map/all_to_all | solution.py:87
  219.2 87.3 %reduce-scatter.5.cloned.1.call-start = ((), (), s32[]{:S(2)}) async-start(), calls=%async_computation.8 | async-start | bytes 1069056 | tf_op jit(solution)/shard_map/reduce_scatter | solution.py:109
  263.9 4.0 %copy-start.10 = (bf16[1280,3584]{1,0:T(8,128)(2,1)}, bf16[1280,3584]{1,0:T(8,128)(2,1)S(1)}, u32[]{:S(2)}) copy-start(bf16[1280,3584]{1,0:T(8,128)(2,1)S(1)} %slice_dynamic-update-slice_fusion) | copy-start | bytes 27525124
  268.0 1.9 copy-start.2
  271.5 7.2 %slice-start = ((s8[9175040]{0:T(1024)(128)(4,1)}), s8[786432]{0:T(1024)(128)(4,1)S(1)}, s32[]{:S(2)}) async-start(s8[9175040]{0:T(1024)(128)(4,1)} %bitcast.90), calls=%async_computation.9 | async-start | bytes 1572864
  271.5 7.2 %copy-start.7 = (f32[1280,224]{0,1:T(8,128)S(1)}, f32[1280,224]{0,1:T(8,128)}, u32[]{:S(2)}) copy-start(f32[1280,224]{0,1:T(8,128)} %copy-done.6) | copy-start | bytes 3440644
  271.6 7.2 %slice-start.1 = ((s8[9175040]{0:T(1024)(128)(4,1)}), s8[4194304]{0:T(1024)(128)(4,1)S(1)}, s32[]{:S(2)}) async-start(s8[9175040]{0:T(1024)(128)(4,1)} %bitcast.90), calls=%async_computation.10 | async-start | bytes 8388608
  271.6 7.2 %slice-start.2 = ((s8[9175040]{0:T(1024)(128)(4,1)}), s8[4194304]{0:T(1024)(128)(4,1)S(1)}, s32[]{:S(2)}) async-start(s8[9175040]{0:T(1024)(128)(4,1)} %bitcast.90), calls=%async_computation.11 | async-start | bytes 8388608
  271.6 7.2 %copy-start.14 = (f32[1280,224]{0,1:T(8,128)S(1)}, f32[1280,224]{0,1:T(8,128)}, u32[]{:S(2)}) copy-start(f32[1280,224]{0,1:T(8,128)} %fusion.10) | copy-start | bytes 3440644
  278.8 3.5 %copy-start.5 = (f32[1280,224]{0,1:T(8,128)S(1)}, f32[1280,224]{0,1:T(8,128)}, u32[]{:S(2)}) copy-start(f32[1280,224]{0,1:T(8,128)} %copy-done.4) | copy-start | bytes 3440644
Sparse Core Ops, SparseCore 0:
  61.6 54.3 all-gather.2
  139.2 58.9 reduce-scatter.2
  200.6 55.1 all-gather.4
  271.7 34.7 reduce-scatter.4
